TPU v7x, 32 devices: a whole 2x2x4 slice. The times are simulated.
32 devices in a mesh: groups: 2 (over y), tensor: 8 (over z, x), dp: 2 (over core).
Axes of the slice: x: 2, y: 2, z: 4, core: 2. Of those that a mesh axis runs over, the one named last changes fastest.
Arguments:
- hidden: bfloat16 [2400, 8192], P(('groups', 'dp'), 'tensor'), parts along dimension 0, may hold values from -6 to 6
- norm_gain: float32 [8192], replicated, may hold values from 0.1 to 1.9
- query_weight: bfloat16 [8192, 8192], P('dp', 'tensor'), may hold values from -0.09375 to 0.09375
- query_keep: int32 [128, 128], P('dp', 'tensor'), may hold values 0 or 1
- kv_weight: bfloat16 [2048, 8192], P('tensor', 'dp'), may hold values from -0.0625 to 0.0625
- out_weight: bfloat16 [8192, 8192], P('tensor', 'dp'), may hold values from -0.5 to 0.5
- out_keep: int32 [128, 128], P('tensor', 'dp'), may hold values 0 or 1
- pair_lengths: int32 [4, 4], P(('groups', 'dp')), parts along dimension 0, may hold values from 1 to 300, 600 in all within a row
- premise_lengths: int32 [4, 4], P(('groups', 'dp')), parts along dimension 0, may hold values from 1 to 299
Outputs:
- attn_out: bfloat16 [2400, 8192], P(('groups', 'dp'), 'tensor'), parts along dimension 0
There are 2 independent parts, one for each index of `groups`. A program takes and returns all parts, laid end to end along the dimension named above; an argument that names none is the same for every part. Nothing has to cross between parts.
Inputs may be any that keep to these rules, and one draw needn't show every extreme that they name: `pair_lengths`: each row lists the 4 pair lengths of one batch in order; they sum to 600.
All inputs are finite; a program needn't handle non-finite values. No bound on the sum of `query_keep` or of `out_keep` on one device may be relied on, other than what follows from the above.
Results may differ from a plain program's by a relative error of at most 0.01.
Values may be sent and summed in bfloat16 or wider, within the bound.
No kernel may reach another device: no remote copies, remote signals or barrier semaphores. Data moves between devices by JAX's collectives and lax.ppermute only.
A program may use at most 192 MiB of HBM per device.

v0:
```python
import jax
import jax.numpy as jnp
from jax import lax
from jax.sharding import PartitionSpec as P

HEADS = 64
KVH = 8
HD = 128


def rotate_pairs(values, positions):
    half_width = values.shape[-1] // 2
    inverse = 500000.0 ** (-(jnp.arange(half_width, dtype=jnp.float32) * 2.0 / values.shape[-1]))
    angles = positions[:, None] * inverse[None, :]
    cosine = jnp.cos(angles)[:, None, :]
    sine_part = jnp.sin(angles)[:, None, :]
    first_half = values[..., :half_width]
    second_half = values[..., half_width:]
    return jnp.concatenate(
        [
            first_half * cosine - second_half * sine_part,
            second_half * cosine + first_half * sine_part,
        ],
        axis=-1,
    )


def pair_layout(lengths, premise, count):
    pair_ends = jnp.cumsum(lengths)
    pair_starts = pair_ends - lengths
    position = jnp.arange(count, dtype=jnp.int32)
    pair_index = jnp.sum((position[:, None] >= pair_ends[None, :]).astype(jnp.int32), axis=1)
    one_hot = (
        pair_index[:, None] == jnp.arange(lengths.shape[0], dtype=jnp.int32)[None, :]
    ).astype(jnp.int32)
    offset = position - jnp.sum(one_hot * pair_starts[None, :], axis=1)
    premise_used = jnp.minimum(premise, lengths - 1)
    in_premise = offset < jnp.sum(one_hot * premise_used[None, :], axis=1)
    allowed = (pair_index[:, None] == pair_index[None, :]) & (
        in_premise[None, :] | jnp.logical_not(in_premise)[:, None]
    )
    return (offset.astype(jnp.float32), allowed)


def prune(weight, keep):
    blocks = weight.reshape(
        keep.shape[0],
        weight.shape[0] // keep.shape[0],
        keep.shape[1],
        weight.shape[1] // keep.shape[1],
    )
    blocks = blocks * keep.astype(weight.dtype)[:, None, :, None]
    return blocks.reshape(weight.shape)


def on_device(
    hidden,
    norm_gain,
    query_weight,
    query_keep,
    kv_weight,
    out_weight,
    out_keep,
    pair_lengths,
    premise_lengths,
):
    tensor_rank = lax.axis_index("tensor")
    total_rows = hidden.shape[0]
    head_local = query_weight.shape[1] // HD
    query_pruned = prune(query_weight, query_keep)
    out_pruned = prune(out_weight, out_keep)
    query_full = lax.all_gather(query_pruned, "dp", axis=0, tiled=True)
    kv_full, out_full = (
        lax.all_gather(kv_weight, "dp", axis=1, tiled=True),
        lax.all_gather(out_pruned, "dp", axis=1, tiled=True),
    )
    whole = lax.all_gather(hidden, "tensor", axis=1, tiled=True)
    rows_float = whole.astype(jnp.float32)
    mean_square = jnp.mean(rows_float * rows_float, axis=-1, keepdims=True)
    normed = (rows_float * lax.rsqrt(mean_square + 1e-05) * norm_gain).astype(jnp.bfloat16)
    queries_raw = jnp.dot(normed, query_full, preferred_element_type=jnp.float32)
    kv_piece = lax.dot_general(
        normed, kv_full, (((1,), (1,)), ((), ())), preferred_element_type=jnp.float32
    ).astype(jnp.bfloat16)
    kv_whole = lax.all_gather(kv_piece, "tensor", axis=1, tiled=True)
    offsets, allowed = pair_layout(pair_lengths[0], premise_lengths[0], total_rows)
    queries = rotate_pairs(queries_raw.reshape(total_rows, head_local, HD), offsets).astype(
        jnp.bfloat16
    )
    keys_all = rotate_pairs(
        kv_whole[:, : KVH * HD].reshape(total_rows, KVH, HD).astype(jnp.float32), offsets
    ).astype(jnp.bfloat16)
    values_all = kv_whole[:, KVH * HD :].reshape(total_rows, KVH, HD)
    chosen = (tensor_rank * head_local + jnp.arange(head_local, dtype=jnp.int32)) // (HEADS // KVH)
    keys_used = jnp.take(keys_all, chosen, axis=1)
    values_used = jnp.take(values_all, chosen, axis=1)
    count_blocks = total_rows // total_rows
    scale = HD ** (-0.5)

    def attend(operands):
        query_block, allowed_block = operands
        scores = (
            jnp.einsum("qhd,khd->hqk", query_block, keys_used, preferred_element_type=jnp.float32)
            * scale
        )
        weighted = jnp.where(allowed_block[None, :, :], jnp.exp(scores), 0.0)
        probs = (weighted / jnp.sum(weighted, axis=-1, keepdims=True)).astype(jnp.bfloat16)
        return jnp.einsum(
            "hqk,khd->qhd", probs, values_used, preferred_element_type=jnp.float32
        ).astype(jnp.bfloat16)

    context = lax.map(
        attend,
        (
            queries.reshape(count_blocks, total_rows, head_local, HD),
            allowed.reshape(count_blocks, total_rows, total_rows),
        ),
    )
    context = context.reshape(total_rows, head_local * HD)
    terms = jnp.dot(context, out_full, preferred_element_type=jnp.float32)
    mixed = lax.psum_scatter(terms, "tensor", scatter_dimension=1, tiled=True)
    return mixed.astype(jnp.bfloat16)


def solution(mesh):
    placed = (
        P(("groups", "dp"), "tensor"),
        P(),
        P("dp", "tensor"),
        P("dp", "tensor"),
        P("tensor", "dp"),
        P("tensor", "dp"),
        P("tensor", "dp"),
        P(("groups", "dp"), None),
        P(("groups", "dp"), None),
    )
    return jax.shard_map(
        on_device,
        mesh=mesh,
        in_specs=placed,
        out_specs=P(("groups", "dp"), "tensor"),
        check_vma=False,
    )
```

profile of v0, /device:TPU:0, one launch (start us, length us, event | category | flops | bytes accessed | tf_op | source)
XLA Modules:
  0.0 643.1 jit_solution(441192260038344043)
XLA Ops:
  6.5 0.0 copy-start.1
  6.5 0.0 all-gather.6.cloned.1.call-start
  6.5 0.7 all-gather.6.cloned.1.call-update
  7.3 0.0 all-gather.8.cloned.1.call-start
  7.3 0.7 all-gather.8.cloned.1.call-update
  8.0 0.0 all-gather.12.cloned.1.call-start
  8.1 0.0 copy-done.1
  8.1 0.1 copy.25
  8.2 6.2 mul.162
  14.4 22.8 %mul.163 = bf16[4096,1024]{1,0:T(8,128)(2,1)} reshape(bf16[64,64,16,64]{3,2,1,0:T(8,128)(2,1)} %mul.162) | data formatting | bytes 16777216 | tf_op jit(solution)/shard_map/mul | solution.py:52
  37.2 10.7 %mul.164 = bf16[4096,1024]{1,0:T(8,128)(2,1)} multiply(bf16[4096,1024]{1,0:T(8,128)(2,1)} %param.13, bf16[4096,1024]{1,0:T(8,128)(2,1)} %mul.163) | non-fusion elementwise | flops 4194304 | bytes 25165824 | tf_op jit(solution)/shard_map/mul | solution.py:52
  47.9 0.0 all-gather.12.cloned.1.call-update
  47.9 0.0 copy-start.5
  47.9 0.0 all-gather.10.cloned.1.call-start
  48.0 106.5 %all-gather.6.cloned.1.call-done = bf16[600,8192]{1,0:T(8,128)(2,1)} async-done(((bf16[600,1024]{1,0:T(8,128)(2,1)}), bf16[600,8192]{1,0:T(8,128)(2,1)}) %all-gather.6.cloned.1.call-update) | async-done | bytes 9830416 | tf_op jit(solution)/shard_map/all_gather | solution.py:77
  154.5 5.8 fusion
  160.3 0.0 copy-start.2
  160.3 7.7 %all-gather.8.cloned.1.call-done = bf16[256,8192]{1,0:T(8,128)(2,1)} async-done(((bf16[256,4096]{1,0:T(8,128)(2,1)}), bf16[256,8192]{1,0:T(8,128)(2,1)}) %all-gather.8.cloned.1.call-update) | async-done | bytes 4194320 | tf_op jit(solution)/shard_map/all_gather | solution.py:74
  168.0 0.0 copy-done.5
  168.0 8.6 %fusion.27 = bf16[600,256]{1,0:T(8,128)(2,1)} fusion(bf16[256,8192]{1,0:T(8,128)(2,1)} %all-gather.8.cloned.1.call-done, bf16[600,8192]{1,0:T(8,128)(2,1)} %all-gather.6.cloned.1.call-done, f32[8192]{0:T(1024)S(1)} %copy-done.5, f32[600]{0:T(1024)S(1)} %add_rsqrt_fusion), kind=kOutput, calls=%fused_computation.38 | convolution fusion | flops 2536396800 | bytes 14367072 | tf_op jit(solution)/shard_map/dot_general | solution.py:82
  176.6 0.0 all-gather.10.cloned.1.call-update
  176.6 0.0 all-gather.14.cloned.1.call-start
  176.7 0.0 copy-done.2
  176.7 10.6 %mul.179 = bf16[16,64,64,64]{3,2,1,0:T(8,128)(2,1)} broadcast(bf16[16,64]{1,0:T(8,128)(2,1)S(1)} %convert_element_type.59), dimensions={0,2} | broadcast | bytes 8390656 | tf_op jit(solution)/shard_map/mul | solution.py:52
  187.3 23.1 %mul.180 = bf16[1024,4096]{1,0:T(8,128)(2,1)} reshape(bf16[16,64,64,64]{3,2,1,0:T(8,128)(2,1)} %mul.179) | data formatting | bytes 16777216 | tf_op jit(solution)/shard_map/mul | solution.py:52
  210.4 10.3 %mul.181 = bf16[1024,4096]{1,0:T(8,128)(2,1)} multiply(bf16[1024,4096]{1,0:T(8,128)(2,1)} %param.16, bf16[1024,4096]{1,0:T(8,128)(2,1)} %mul.180) | non-fusion elementwise | flops 4194304 | bytes 25165824 | tf_op jit(solution)/shard_map/mul | solution.py:52
  220.7 0.0 copy-start.3
  220.7 0.0 copy-start.4
  220.7 0.0 all-gather.14.cloned.1.call-update
  220.8 0.2 reduce-scatter.2.cloned.1.call-start
  221.0 0.4 copy-done.3
  221.4 0.2 reduce-window.4
  221.6 0.1 convert_reduce_fusion
  221.7 0.0 copy-done.4
  221.7 0.1 select_reduce_fusion
  221.9 0.4 or_and_fusion
  222.2 1.1 multiply_cosine_fusion
  223.4 0.0 all-gather.12.cloned.1.call-done
  223.4 15.6 %fusion.9 = f32[75,8,8,128]{3,1,2,0:T(8,128)S(1)} fusion(bf16[8192,1024]{1,0:T(8,128)(2,1)} %all-gather.12.cloned.1.call-done, bf16[600,8192]{1,0:T(8,128)(2,1)} %all-gather.6.cloned.1.call-done, f32[8192]{0:T(1024)S(1)} %copy-done.5, f32[600]{0:T(1024)S(1)} %add_rsqrt_fusion), kind=kOutput, calls=%fused_computation.18 | convolution fusion | flops 10085990400 | bytes 29100384 | tf_op jit(solution)/shard_map/dot_general | solution.py:81
  239.0 0.6 copy.39
  239.6 19.9 %all-gather.10.cloned.1.call-done = bf16[600,2048]{1,0:T(8,128)(2,1)} async-done(((bf16[600,256]{1,0:T(8,128)(2,1)}), bf16[600,2048]{1,0:T(8,128)(2,1)}) %all-gather.10.cloned.1.call-update) | async-done | bytes 2457616 | tf_op jit(solution)/shard_map/all_gather | solution.py:85
  259.4 2.1 slice_bitcast_fusion
  261.5 0.6 copy.40
  262.1 1.3 copy.54
  263.4 1.9 fusion.42
  265.3 2.9 subtract_convert_fusion
  268.1 0.0 copy-start
  268.1 0.7 pad_maximum_fusion
  268.8 1.7 gather_fusion.1
  270.5 0.0 copy-done
  270.5 0.8 gather_fusion
  271.3 6.8 %fusion.3 = (f32[8,600]{1,0:T(8,128)S(1)}, f32[8,600,600]{1,2,0:T(8,128)S(1)}) fusion(pred[600,600]{0,1:T(8,128)(4,1)S(1)} %or_and_fusion, bf16[8,600,128]{2,1,0:T(8,128)(2,1)} %gather_fusion.1, pred[8]{0:T(512)(128)(4,1)S(1)} %compare_and_fusion, bf16[600,8,64]{2,0,1:T(8,128)(2,1)} %get-tuple-element.38, bf16[600,8,64]{2,0,1:T(8,128)(2,1)} %get-tuple-element.39), kind=kOutput, calls=%fused_computation.9 | convolution fusion | flops 748987200 | bytes 14356808 | tf_op jit(solution)/shard_map/while/body/eval_jaxpr/qhd,khd->hqk/dot_general | solution.py:103
  278.1 4.4 fusion.13
  282.6 6.6 %all-gather.14.cloned.1.call-done = bf16[1024,8192]{1,0:T(8,128)(2,1)} async-done(((bf16[1024,4096]{1,0:T(8,128)(2,1)}), bf16[1024,8192]{1,0:T(8,128)(2,1)}) %all-gather.14.cloned.1.call-update) | async-done | bytes 16777232 | tf_op jit(solution)/shard_map/all_gather | solution.py:75
  289.2 17.6 %fusion.14 = f32[600,8192]{1,0:T(8,128)} fusion(bf16[1024,8192]{1,0:T(8,128)(2,1)} %all-gather.14.cloned.1.call-done, bf16[8,75,8,128]{3,2,1,0:T(8,128)(2,1)S(1)} %fusion.13), kind=kOutput, calls=%fused_computation.22 | convolution fusion | flops 10066329600 | bytes 37666816 | tf_op jit(solution)/shard_map/dot_general | solution.py:120
  306.8 0.0 reduce-scatter.2.cloned.1.call-update
  306.8 326.6 %reduce-scatter.2.cloned.1.call-done = f32[600,1024]{1,0:T(8,128)} async-done(((f32[600,8192]{1,0:T(8,128)}), f32[600,1024]{1,0:T(8,128)}) %reduce-scatter.2.cloned.1.call-update) | async-done | bytes 2457616 | tf_op jit(solution)/shard_map/reduce_scatter | solution.py:121
  633.4 2.9 convert_element_type.60
  (10 shorter events, 0.1 us)
Async XLA Ops:
  6.5 1.5 copy-start.1
  6.5 148.0 %all-gather.6.cloned.1.call-start = ((), (), s32[]{:S(2)}) async-start(), calls=%async_computation.1 | async-start | bytes 11059200 | tf_op jit(solution)/shard_map/all_gather | solution.py:77
  7.3 160.7 %all-gather.8.cloned.1.call-start = ((), (), s32[]{:S(2)}) async-start(), calls=%async_computation.2 | async-start | bytes 6291456 | tf_op jit(solution)/shard_map/all_gather | solution.py:74
  8.0 215.4 %all-gather.12.cloned.1.call-start = ((), (), s32[]{:S(2)}) async-start(), calls=%async_computation.4 | async-start | bytes 25165824 | tf_op jit(solution)/shard_map/all_gather | solution.py:72
  47.9 120.1 %copy-start.5 = (f32[8192]{0:T(1024)S(1)}, f32[8192]{0:T(1024)}, u32[]{:S(2)}) copy-start(f32[8192]{0:T(1024)} %param.12) | copy-start | bytes 98308
  47.9 211.5 %all-gather.10.cloned.1.call-start = ((), (), s32[]{:S(2)}) async-start(), calls=%async_computation.3 | async-start | bytes 2764800 | tf_op jit(solution)/shard_map/all_gather | solution.py:85
  160.3 16.4 %copy-start.2 = (s32[16,64]{1,0:T(8,128)S(1)}, s32[16,64]{1,0:T(8,128)}, u32[]{:S(2)}) copy-start(s32[16,64]{1,0:T(8,128)} %param.17) | copy-start | bytes 12292
  176.6 112.5 %all-gather.14.cloned.1.call-start = ((), (), s32[]{:S(2)}) async-start(), calls=%async_computation.5 | async-start | bytes 25165824 | tf_op jit(solution)/shard_map/all_gather | solution.py:75
  220.7 0.7 copy-start.3
  220.7 1.0 copy-start.4
  220.8 412.6 %reduce-scatter.2.cloned.1.call-start = ((), (), s32[]{:S(2)}) async-start(), calls=%async_computation.6 | async-start | bytes 22118400 | tf_op jit(solution)/shard_map/reduce_scatter | solution.py:121
  268.1 2.4 copy-start
Sparse Core Ops, SparseCore 0:
  9.5 144.9 all-gather.5
  156.0 11.8 all-gather.7
  169.5 31.1 all-gather.11
  202.6 56.7 all-gather.9
  260.8 28.2 all-gather.13
  306.9 326.4 reduce-scatter.1
where the time goes:
time: 644 us; the launch traced here: 643 us
  waiting for transfers between devices  469 us (73%)
  local copies, waits for them, and re-layouts  70 us (11%)
  matrix products  53 us (8%)
  other arithmetic  37.3 us (6%)
  between operations  13.7 us (2%)
    reduce_scatter x1, waiting for transfers between devices, on_device(): mixed = lax.psum_scatter(terms, 'tensor', scatter_dimension=1, tiled=True)  327 us
    all_gather x1, waiting for transfers between devices, on_device(): whole = lax.all_gather(hidden, 'tensor', axis=1, tiled=True)  107 us
    mul x4, local copies, waits for them, and re-layouts, prune(): blocks = blocks * keep.astype(weight.dtype)[:, None, :, None]  62.7 us
    mul x2, other arithmetic, prune(): blocks = blocks * keep.astype(weight.dtype)[:, None, :, None]  21 us
    all_gather x1, waiting for transfers between devices, on_device(): kv_whole = lax.all_gather(kv_piece, 'tensor', axis=1, tiled=True)  19.9 us
    dot_general x1, matrix products, on_device(): terms = jnp.dot(context, out_full, preferred_element_type=jnp.float32)  17.6 us
    dot_general x1, matrix products, on_device(): jnp.dot(normed, query_full, preferred_element_type=jnp.float32)  15.6 us
  transfers between devices with their start and end apart: 6, of which 5 were waited for; matrix products, arithmetic and copies ran while one was open for 22% of the time, Pallas kernels for 0%

commit v1 on v0

--- a/solution.py
+++ b/solution.py
@@ -1,5 +1,6 @@
 import jax
 import jax.numpy as jnp
+import numpy as np
 from jax import lax
 from jax.sharding import PartitionSpec as P
 
@@ -53,7 +54,139 @@
     return blocks.reshape(weight.shape)
 
 
-def on_device(
+def ring_order(z_size, x_size):
+    if x_size == 1 or z_size == 1:
+        return list(range(z_size * x_size))
+    cycle = [(z, 0) for z in range(z_size)]
+    for step, z in enumerate(range(z_size - 1, -1, -1)):
+        xs = list(range(1, x_size))
+        cycle += [(z, x) for x in (xs if step % 2 == 0 else xs[::-1])]
+    return [z * x_size + x for z, x in cycle]
+
+
+def make_fast(n, order):
+    position_of = np.zeros(n, np.int32)
+    for p, t in enumerate(order):
+        position_of[t] = p
+    order_arr = np.asarray(order, np.int32)
+    to_next = [(order[i], order[(i + 1) % n]) for i in range(n)]
+    to_prev = [(order[i], order[(i - 1) % n]) for i in range(n)]
+    n_cw = n // 2
+    n_ccw = (n - 1) // 2
+
+    def on_device(
+        hidden,
+        norm_gain,
+        query_weight,
+        query_keep,
+        kv_weight,
+        out_weight,
+        out_keep,
+        pair_lengths,
+        premise_lengths,
+    ):
+        tensor_rank = lax.axis_index("tensor")
+        dp_rank = lax.axis_index("dp")
+        pos = jnp.asarray(position_of)[tensor_rank]
+        ring = jnp.asarray(order_arr)
+        total_rows, feat = hidden.shape
+        head_local = query_weight.shape[1] // HD
+        half_rows = query_weight.shape[0]
+
+        query_mine = prune(query_weight, query_keep)
+        out_mine = prune(out_weight, out_keep)
+        swap = [(0, 1), (1, 0)]
+        query_other = lax.ppermute(query_mine, "dp", swap)
+        kv_other = lax.ppermute(kv_weight, "dp", swap)
+        out_other = lax.ppermute(out_mine, "dp", swap)
+
+        whole = jnp.zeros((total_rows, n * feat), hidden.dtype)
+        whole = lax.dynamic_update_slice(whole, hidden, (0, tensor_rank * feat))
+        fwd = hidden
+        for s in range(n_cw):
+            fwd = lax.ppermute(fwd, "tensor", to_next)
+            src = ring[(pos - s - 1) % n]
+            whole = lax.dynamic_update_slice(whole, fwd, (0, src * feat))
+        bwd = hidden
+        for s in range(n_ccw):
+            bwd = lax.ppermute(bwd, "tensor", to_prev)
+            src = ring[(pos + s + 1) % n]
+            whole = lax.dynamic_update_slice(whole, bwd, (0, src * feat))
+
+        rows_float = whole.astype(jnp.float32)
+        mean_square = jnp.mean(rows_float * rows_float, axis=-1, keepdims=True)
+        normed = (rows_float * lax.rsqrt(mean_square + 1e-05) * norm_gain).astype(jnp.bfloat16)
+        mine_cols = lax.dynamic_slice_in_dim(normed, dp_rank * half_rows, half_rows, axis=1)
+        other_cols = lax.dynamic_slice_in_dim(normed, (1 - dp_rank) * half_rows, half_rows, axis=1)
+
+        queries_raw = jnp.dot(mine_cols, query_mine, preferred_element_type=jnp.float32) + jnp.dot(
+            other_cols, query_other, preferred_element_type=jnp.float32
+        )
+        contract = (((1,), (1,)), ((), ()))
+        kv_piece = (
+            lax.dot_general(mine_cols, kv_weight, contract, preferred_element_type=jnp.float32)
+            + lax.dot_general(other_cols, kv_other, contract, preferred_element_type=jnp.float32)
+        ).astype(jnp.bfloat16)
+
+        low = tensor_rank < n // 2
+        first = kv_piece[:, :HD]
+        second = kv_piece[:, HD:]
+        pairs_a = [(s, 2 * s) if s < n // 2 else (s, 2 * (s - n // 2) + 1) for s in range(n)]
+        pairs_b = [(s, 2 * s + 1) if s < n // 2 else (s, 2 * (s - n // 2)) for s in range(n)]
+        got_a = lax.ppermute(jnp.where(low, first, second), "tensor", pairs_a)
+        got_b = lax.ppermute(jnp.where(low, second, first), "tensor", pairs_b)
+        even = tensor_rank % 2 == 0
+        key_head = jnp.where(even, got_a, got_b)
+        value_head = jnp.where(even, got_b, got_a)
+
+        offsets, allowed = pair_layout(pair_lengths[0], premise_lengths[0], total_rows)
+        queries = rotate_pairs(queries_raw.reshape(total_rows, head_local, HD), offsets).astype(
+            jnp.bfloat16
+        )
+        keys = rotate_pairs(key_head.astype(jnp.float32)[:, None, :], offsets)[:, 0, :].astype(
+            jnp.bfloat16
+        )
+        scale = HD ** (-0.5)
+        scores = jnp.einsum("qhd,kd->hqk", queries, keys, preferred_element_type=jnp.float32) * scale
+        weighted = jnp.where(allowed[None, :, :], jnp.exp(scores), 0.0)
+        probs = (weighted / jnp.sum(weighted, axis=-1, keepdims=True)).astype(jnp.bfloat16)
+        context = jnp.einsum(
+            "hqk,kd->qhd", probs, value_head, preferred_element_type=jnp.float32
+        ).astype(jnp.bfloat16)
+        context = context.reshape(total_rows, head_local * HD)
+
+        terms_mine = jnp.dot(context, out_mine, preferred_element_type=jnp.float32)
+        terms_other = jnp.dot(context, out_other, preferred_element_type=jnp.float32)
+        terms = jnp.where(
+            dp_rank == 0,
+            jnp.concatenate([terms_mine, terms_other], axis=1),
+            jnp.concatenate([terms_other, terms_mine], axis=1),
+        )
+
+        def chunk(dest_pos):
+            return lax.dynamic_slice_in_dim(terms, ring[dest_pos % n] * feat, feat, axis=1)
+
+        total = chunk(pos)
+        acc = None
+        for s in range(n_cw):
+            part = chunk(pos + n_cw - s)
+            send = part if acc is None else part + acc.astype(jnp.float32)
+            acc = lax.ppermute(send.astype(jnp.bfloat16), "tensor", to_next)
+        if acc is not None:
+            total = total + acc.astype(jnp.float32)
+        acc = None
+        for s in range(n_ccw):
+            part = chunk(pos - (n_ccw - s))
+            send = part if acc is None else part + acc.astype(jnp.float32)
+            acc = lax.ppermute(send.astype(jnp.bfloat16), "tensor", to_prev)
+        if acc is not None:
+            total = total + acc.astype(jnp.float32)
+        return total.astype(jnp.bfloat16)
+
+    return on_device
+
+
+def generic(
     hidden,
     norm_gain,
     query_weight,
@@ -94,28 +227,15 @@
     chosen = (tensor_rank * head_local + jnp.arange(head_local, dtype=jnp.int32)) // (HEADS // KVH)
     keys_used = jnp.take(keys_all, chosen, axis=1)
     values_used = jnp.take(values_all, chosen, axis=1)
-    count_blocks = total_rows // total_rows
     scale = HD ** (-0.5)
-
-    def attend(operands):
-        query_block, allowed_block = operands
-        scores = (
-            jnp.einsum("qhd,khd->hqk", query_block, keys_used, preferred_element_type=jnp.float32)
-            * scale
-        )
-        weighted = jnp.where(allowed_block[None, :, :], jnp.exp(scores), 0.0)
-        probs = (weighted / jnp.sum(weighted, axis=-1, keepdims=True)).astype(jnp.bfloat16)
-        return jnp.einsum(
-            "hqk,khd->qhd", probs, values_used, preferred_element_type=jnp.float32
-        ).astype(jnp.bfloat16)
-
-    context = lax.map(
-        attend,
-        (
-            queries.reshape(count_blocks, total_rows, head_local, HD),
-            allowed.reshape(count_blocks, total_rows, total_rows),
-        ),
-    )
+    scores = (
+        jnp.einsum("qhd,khd->hqk", queries, keys_used, preferred_element_type=jnp.float32) * scale
+    )
+    weighted = jnp.where(allowed[None, :, :], jnp.exp(scores), 0.0)
+    probs = (weighted / jnp.sum(weighted, axis=-1, keepdims=True)).astype(jnp.bfloat16)
+    context = jnp.einsum(
+        "hqk,khd->qhd", probs, values_used, preferred_element_type=jnp.float32
+    ).astype(jnp.bfloat16)
     context = context.reshape(total_rows, head_local * HD)
     terms = jnp.dot(context, out_full, preferred_element_type=jnp.float32)
     mixed = lax.psum_scatter(terms, "tensor", scatter_dimension=1, tiled=True)
@@ -134,8 +254,20 @@
         P(("groups", "dp"), None),
         P(("groups", "dp"), None),
     )
+    n = mesh.shape["tensor"]
+    if n == KVH and mesh.shape["dp"] == 2:
+        coords = [getattr(d, "coords", None) for d in mesh.devices.reshape(-1)]
+        z_size, x_size = n, 1
+        if all(c is not None for c in coords):
+            xs = sorted({c[0] for c in coords})
+            zs = sorted({c[2] for c in coords})
+            if len(xs) * len(zs) == n:
+                z_size, x_size = len(zs), len(xs)
+        body = make_fast(n, ring_order(z_size, x_size))
+    else:
+        body = generic
     return jax.shard_map(
-        on_device,
+        body,
         mesh=mesh,
         in_specs=placed,
         out_specs=P(("groups", "dp"), "tensor"),

time: 644 us -> 402 us (0.62)
  waiting for transfers between devices: 469 us -> 171 us
  starting transfers between devices: 0.39 us -> 26.2 us
  other arithmetic: 37.3 us -> 60.8 us
    reduce_scatter x1 -> x0, waiting for transfers between devices: 327 us -> none  [on_device(): mixed = lax.psum_scatter(terms, 'tensor', scatter_dimension=1, tiled=True)]
    ppermute x0 -> x19, waiting for transfers between devices: none -> 171 us  [the longest x4 73.6 us: on_device(): acc = lax.ppermute(send.astype(jnp.bfloat16), 'tensor', to_next)]
    all_gather x5 -> x0, waiting for transfers between devices: 141 us -> none  [the longest x1 107 us: on_device(): whole = lax.all_gather(hidden, 'tensor', axis=1, tiled=True)]
    ppermute x0 -> x19, starting transfers between devices: none -> 26.2 us  [the longest x4 9.74 us: on_device(): acc = lax.ppermute(send.astype(jnp.bfloat16), 'tensor', to_next)]
    select_n x1 -> x2, other arithmetic: 0.01 us -> 16 us  [the longest x1 15.9 us: on_device(): jnp.where(dp_rank == 0, jnp.concatenate([terms_mine, terms_other], axis=1...]
    convert_element_type x1 -> x6, other arithmetic: 2.91 us -> 17.8 us  [the longest x1 11.4 us: on_device(): (rows_float * lax.rsqrt(mean_square + 1e-05) * norm_gain).astype(jnp.bflo...]
    dot_general x5 -> x8, matrix products: 53 us -> 54.3 us  [the longest x1 11.5 us: on_device(): terms_mine = jnp.dot(context, out_mine, preferred_element_type=jnp.float32)]
  transfers between devices with their start and end apart: 6 -> 19, of which waited for: 5 -> 9; matrix products, arithmetic and copies ran while one was open for 22% -> 38% of each run, Pallas kernels for 0% -> 0%
where the time goes in v1:
time: 402 us; the launch traced here: 396 us
  waiting for transfers between devices  171 us (43%)
  local copies, waits for them, and re-layouts  69.6 us (17%)
  other arithmetic  60.8 us (15%)
  matrix products  54.3 us (14%)
  starting transfers between devices  26.2 us (7%)
  between operations  13.6 us (3%)
    ppermute x4, waiting for transfers between devices, on_device(): acc = lax.ppermute(send.astype(jnp.bfloat16), 'tensor', to_next)  73.6 us
    mul x4, local copies, waits for them, and re-layouts, prune(): blocks = blocks * keep.astype(weight.dtype)[:, None, :, None]  57.8 us
    ppermute x4, waiting for transfers between devices, on_device(): fwd = lax.ppermute(fwd, 'tensor', to_next)  48.5 us
    ppermute x3, waiting for transfers between devices, on_device(): acc = lax.ppermute(send.astype(jnp.bfloat16), 'tensor', to_prev)  45.8 us
    mul x2, other arithmetic, prune(): blocks = blocks * keep.astype(weight.dtype)[:, None, :, None]  20.8 us
    select_n x1, other arithmetic, on_device(): jnp.where(dp_rank == 0, jnp.concatenate([terms_mine, terms_other], axis=1...  15.9 us
    dot_general x1, matrix products, on_device(): terms_mine = jnp.dot(context, out_mine, preferred_element_type=jnp.float32)  11.5 us
    convert_element_type x1, other arithmetic, on_device(): (rows_float * lax.rsqrt(mean_square + 1e-05) * norm_gain).astype(jnp.bflo...  11.4 us
  transfers between devices with their start and end apart: 19, of which 9 were waited for; matrix products, arithmetic and copies ran while one was open for 38% of the time, Pallas kernels for 0%

profile of v1, /device:TPU:0, one launch (start us, length us, event | category | flops | bytes accessed | tf_op | source)
XLA Modules:
  0.0 395.9 jit_solution(15756205665189647582)
XLA Ops:
  0.0 3.1 collective-permute-start
  3.1 27.1 %collective-permute-done = bf16[600,1024]{1,0:T(8,128)(2,1)S(1)} collective-permute-done((bf16[600,1024]{1,0:T(8,128)(2,1)}, bf16[600,1024]{1,0:T(8,128)(2,1)S(1)}, u32[]{:S(2)}, u32[]{:S(2)}) %collective-permute-start) | collective-permute-done | bytes 1228832 | tf_op jit(solution)/shard_map/ppermute | solution.py:107
  30.2 1.8 collective-permute-start.1
  32.0 0.2 collective-permute-start.4
  32.2 0.7 convert_element_type.92
  33.0 6.1 %mul.254 = bf16[64,64,16,64]{3,2,1,0:T(8,128)(2,1)} broadcast(bf16[64,16]{1,0:T(8,128)(2,1)S(1)} %copy.28), dimensions={0,2} | broadcast | bytes 8390656 | tf_op jit(solution)/shard_map/mul | solution.py:53
  39.1 22.6 %mul.255 = bf16[4096,1024]{1,0:T(8,128)(2,1)} reshape(bf16[64,64,16,64]{3,2,1,0:T(8,128)(2,1)} %mul.254) | data formatting | bytes 16777216 | tf_op jit(solution)/shard_map/mul | solution.py:53
  61.7 10.6 %mul.256 = bf16[4096,1024]{1,0:T(8,128)(2,1)} multiply(bf16[4096,1024]{1,0:T(8,128)(2,1)} %param.13, bf16[4096,1024]{1,0:T(8,128)(2,1)} %mul.255) | non-fusion elementwise | flops 4194304 | bytes 25165824 | tf_op jit(solution)/shard_map/mul | solution.py:53
  72.3 1.9 collective-permute-start.2
  74.2 0.2 collective-permute-start.5
  74.4 6.6 %mul.268 = bf16[16,64,64,64]{3,2,1,0:T(8,128)(2,1)} broadcast(bf16[16,64]{1,0:T(8,128)(2,1)S(1)} %convert_element_type.96), dimensions={0,2} | broadcast | bytes 8390656 | tf_op jit(solution)/shard_map/mul | solution.py:53
  81.0 22.5 %mul.269 = bf16[1024,4096]{1,0:T(8,128)(2,1)} reshape(bf16[16,64,64,64]{3,2,1,0:T(8,128)(2,1)} %mul.268) | data formatting | bytes 16777216 | tf_op jit(solution)/shard_map/mul | solution.py:53
  103.5 10.2 %mul.270 = bf16[1024,4096]{1,0:T(8,128)(2,1)} multiply(bf16[1024,4096]{1,0:T(8,128)(2,1)} %param.16, bf16[1024,4096]{1,0:T(8,128)(2,1)} %mul.269) | non-fusion elementwise | flops 4194304 | bytes 25165824 | tf_op jit(solution)/shard_map/mul | solution.py:53
  113.7 0.5 collective-permute-start.11
  114.1 0.6 dynamic_slice.66
  122.0 0.7 fusion.59
  127.6 0.2 reduce-window.4
  128.0 1.9 collective-permute-start.3
  129.9 0.4 collective-permute-start.6
  130.3 1.2 broadcast_in_dim.15
  131.7 1.1 multiply_cosine_fusion
  133.0 1.4 constant_dynamic-update-slice_fusion.5
  134.4 1.4 constant_dynamic-update-slice_fusion.4
  135.9 21.4 %collective-permute-done.3 = bf16[600,1024]{1,0:T(8,128)(2,1)S(1)} collective-permute-done((bf16[600,1024]{1,0:T(8,128)(2,1)}, bf16[600,1024]{1,0:T(8,128)(2,1)S(1)}, u32[]{:S(2)}, u32[]{:S(2)}) %collective-permute-start.3) | collective-permute-done | bytes 1228832 | tf_op jit(solution)/shard_map/ppermute | solution.py:107
  157.5 1.4 constant_dynamic-update-slice_fusion.1
  159.2 2.0 fusion
  161.2 1.7 copy-done
  162.9 11.4 %fusion.2 = bf16[600,8192]{1,0:T(8,128)(2,1)} fusion(bf16[600,8192]{1,0:T(8,128)(2,1)} %copy-done, f32[8192]{0:T(1024)S(1)} %copy-done.5, f32[600]{0:T(1024)S(1)} %add_rsqrt_fusion), kind=kLoop, calls=%fused_computation.4 | loop fusion | flops 19660800 | bytes 19695968 | tf_op jit(solution)/shard_map/convert_element_type | solution.py:118
  174.3 5.0 %fusion.7 = f32[600,256]{0,1:T(8,128)S(1)} fusion(bf16[256,4096]{1,0:T(8,128)(2,1)} %collective-permute-done.7, bf16[600,8192]{1,0:T(8,128)(2,1)} %fusion.2, s32[]{:T(128)S(6)} %select_n.195), kind=kOutput, calls=%fused_computation.12 | convolution fusion | flops 1258291200 | bytes 7626756 | tf_op jit(solution)/shard_map/dot_general | solution.py:128
  179.4 0.8 copy-done.2
  180.2 3.8 fusion.28
  184.0 1.7 collective-permute-start.8
  185.8 0.9 collective-permute-start.9
  186.6 0.4 or_and_fusion
  187.0 3.4 collective-permute-done.8
  190.5 0.7 fusion.38
  191.2 7.7 %fusion.5 = f32[600,1024]{1,0:T(8,128)S(1)} fusion(bf16[4096,1024]{1,0:T(8,128)(2,1)} %collective-permute-done.10, bf16[600,8192]{1,0:T(8,128)(2,1)S(1)} %copy-done.2, s32[]{:T(128)S(6)} %select_n.195), kind=kOutput, calls=%fused_computation.10 | convolution fusion | flops 5033164800 | bytes 15761412 | tf_op jit(solution)/shard_map/dot_general | solution.py:122
  198.8 7.7 %add_bitcast_fusion = f32[75,8,8,128]{3,1,2,0:T(8,128)S(1)} fusion(f32[600,1024]{1,0:T(8,128)S(1)} %fusion.5, bf16[4096,1024]{1,0:T(8,128)(2,1)} %mul.256, bf16[600,8192]{1,0:T(8,128)(2,1)S(1)} %copy-done.2, s32[]{:T(128)S(6)} %select_n.194), kind=kOutput, calls=%fused_computation.28 | convolution fusion | flops 5033779200 | bytes 18219012 | tf_op jit(solution)/shard_map/dot_general | solution.py:122
  206.5 0.6 copy.45
  207.1 0.8 fusion.58
  207.8 1.0 subtract_convert_fusion
  208.8 3.8 fusion.3
  212.6 3.7 fusion.16
  216.4 11.5 %fusion.22 = f32[600,4096]{1,0:T(8,128)} fusion(bf16[1024,4096]{1,0:T(8,128)(2,1)} %mul.270, bf16[8,75,8,128]{3,2,1,0:T(8,128)(2,1)S(1)} %fusion.16), kind=kOutput, calls=%fused_computation.35 | convolution fusion | flops 5033164800 | bytes 19447808 | tf_op jit(solution)/shard_map/dot_general | solution.py:158
  227.8 11.2 %fusion.20 = f32[600,4096]{1,0:T(8,128)} fusion(bf16[1024,4096]{1,0:T(8,128)(2,1)} %collective-permute-done.11, bf16[8,75,8,128]{3,2,1,0:T(8,128)(2,1)S(1)} %fusion.16), kind=kOutput, calls=%fused_computation.33 | convolution fusion | flops 5033164800 | bytes 19447808 | tf_op jit(solution)/shard_map/dot_general | solution.py:159
  239.0 15.9 %maximum_select_fusion = f32[600,8192]{1,0:T(8,128)S(1)} fusion(f32[600,4096]{1,0:T(8,128)} %fusion.20, f32[600,4096]{1,0:T(8,128)} %fusion.22, pred[]{:T(512)S(6)} %eq.53), kind=kLoop, calls=%fused_computation.5 | loop fusion | flops 14745600 | bytes 39321600 | tf_op jit(solution)/shard_map/jit(_where)/select_n | solution.py:160
  254.9 0.4 dynamic-slice_convert_fusion.1
  255.3 6.1 %collective-permute-start.12 = (bf16[600,1024]{1,0:T(8,128)(2,1)S(1)}, bf16[600,1024]{1,0:T(8,128)(2,1)S(1)}, u32[]{:S(2)}, u32[]{:S(2)}) collective-permute-start(bf16[600,1024]{1,0:T(8,128)(2,1)S(1)} %get-tuple-element.11), channel_id=1, source_target_pairs={{0,4},{4,8},{8,12},{12,14},{14,10},{10,6},{6,2},{2,0},{1,5},{5,9},... | collective-permute-start | bytes 3686408 | tf_op jit(solution)/shard_map/ppermute | solution.py:174
  261.4 24.8 %collective-permute-done.12 = bf16[600,1024]{1,0:T(8,128)(2,1)S(1)} collective-permute-done((bf16[600,1024]{1,0:T(8,128)(2,1)S(1)}, bf16[600,1024]{1,0:T(8,128)(2,1)S(1)}, u32[]{:S(2)}, u32[]{:S(2)}) %collective-permute-start.12) | collective-permute-done | bytes 1228832 | tf_op jit(solution)/shard_map/ppermute | solution.py:174
  286.3 0.5 add_convert_fusion.5
  286.7 1.9 collective-permute-start.13
  288.7 0.2 collective-permute-start.16
  288.8 24.6 %collective-permute-done.13 = bf16[600,1024]{1,0:T(8,128)(2,1)S(1)} collective-permute-done((bf16[600,1024]{1,0:T(8,128)(2,1)S(1)}, bf16[600,1024]{1,0:T(8,128)(2,1)S(1)}, u32[]{:S(2)}, u32[]{:S(2)}) %collective-permute-start.13) | collective-permute-done | bytes 1228832 | tf_op jit(solution)/shard_map/ppermute | solution.py:174
  313.5 0.5 add_convert_fusion.4
  313.9 1.2 collective-permute-start.14
  315.1 24.1 %collective-permute-done.14 = bf16[600,1024]{1,0:T(8,128)(2,1)S(1)} collective-permute-done((bf16[600,1024]{1,0:T(8,128)(2,1)S(1)}, bf16[600,1024]{1,0:T(8,128)(2,1)S(1)}, u32[]{:S(2)}, u32[]{:S(2)}) %collective-permute-start.14) | collective-permute-done | bytes 1228832 | tf_op jit(solution)/shard_map/ppermute | solution.py:174
  339.2 0.9 add_convert_fusion.3
  340.2 1.5 collective-permute-start.17
  341.7 0.6 collective-permute-start.15
  342.3 23.6 %collective-permute-done.17 = bf16[600,1024]{1,0:T(8,128)(2,1)S(1)} collective-permute-done((bf16[600,1024]{1,0:T(8,128)(2,1)S(1)}, bf16[600,1024]{1,0:T(8,128)(2,1)S(1)}, u32[]{:S(2)}, u32[]{:S(2)}) %collective-permute-start.17) | collective-permute-done | bytes 1228832 | tf_op jit(solution)/shard_map/ppermute | solution.py:181
  365.9 0.4 add_convert_fusion.1
  366.3 2.3 collective-permute-start.18
  369.2 22.1 %collective-permute-done.18 = bf16[600,1024]{1,0:T(8,128)(2,1)} collective-permute-done((bf16[600,1024]{1,0:T(8,128)(2,1)S(1)}, bf16[600,1024]{1,0:T(8,128)(2,1)}, u32[]{:S(2)}, u32[]{:S(2)}) %collective-permute-start.18) | collective-permute-done | bytes 1228832 | tf_op jit(solution)/shard_map/ppermute | solution.py:181
  391.4 4.1 %add_convert_fusion = bf16[600,1024]{1,0:T(8,128)(2,1)} fusion(bf16[600,1024]{1,0:T(8,128)(2,1)} %collective-permute-done.18, bf16[600,1024]{1,0:T(8,128)(2,1)} %collective-permute-done.15, f32[600,8192]{1,0:T(8,128)} %copy-done.1, s32[]{:T(128)S(6)} %select_n.204), kind=kLoop, calls=%fused_computation.18 | loop fusion | flops 3072000 | bytes 6144004 | tf_op jit(solution)/shard_map/convert_element_type | solution.py:184
  (47 shorter events, 1.2 us)
Async XLA Ops:
  0.0 30.2 %collective-permute-start = (bf16[600,1024]{1,0:T(8,128)(2,1)}, bf16[600,1024]{1,0:T(8,128)(2,1)S(1)}, u32[]{:S(2)}, u32[]{:S(2)}) collective-permute-start(bf16[600,1024]{1,0:T(8,128)(2,1)} %param.11), channel_id=1, source_target_pairs={{0,4},{4,8},{8,12},{12,14},{14,10},{10,6},{6,2},{2,0},{1,5},{5,9},... | collective-permute-start | bytes 3686408 | tf_op jit(solution)/shard_map/ppermute | solution.py:107
  30.2 42.1 %collective-permute-start.1 = (bf16[600,1024]{1,0:T(8,128)(2,1)S(1)}, bf16[600,1024]{1,0:T(8,128)(2,1)}, u32[]{:S(2)}, u32[]{:S(2)}) collective-permute-start(bf16[600,1024]{1,0:T(8,128)(2,1)S(1)} %collective-permute-done), channel_id=1, source_target_pairs={{0,4},{4,8},{8,12},{12,14},{14,10},{10,6},{6,2},{2,0},{1,5},{5,9},... | collective-permute-start | bytes 3686408 | tf_op jit(solution)/shard_map/ppermute | solution.py:107
  32.0 42.2 %collective-permute-start.4 = (bf16[600,1024]{1,0:T(8,128)(2,1)}, bf16[600,1024]{1,0:T(8,128)(2,1)S(1)}, u32[]{:S(2)}, u32[]{:S(2)}) collective-permute-start(bf16[600,1024]{1,0:T(8,128)(2,1)} %param.11), channel_id=1, source_target_pairs={{0,2},{4,0},{8,4},{12,8},{14,12},{10,14},{6,10},{2,6},{1,3},{5,1},... | collective-permute-start | bytes 3686408 | tf_op jit(solution)/shard_map/ppermute | solution.py:112
  61.7 12.7 %copy-start.6 = (s32[16,64]{1,0:T(8,128)S(1)}, s32[16,64]{1,0:T(8,128)}, u32[]{:S(2)}) copy-start(s32[16,64]{1,0:T(8,128)} %param.17) | copy-start | bytes 12292
  72.3 118.9 %collective-permute-start.10 = (bf16[4096,1024]{1,0:T(8,128)(2,1)}, bf16[4096,1024]{1,0:T(8,128)(2,1)}, u32[]{:S(2)}, u32[]{:S(2)}) collective-permute-start(bf16[4096,1024]{1,0:T(8,128)(2,1)} %mul.256), channel_id=1, source_target_pairs={{0,1},{1,0},{2,3},{3,2},{4,5},{5,4},{6,7},{7,6},{8,9},{9,8},{10,11... | collective-permute-start | bytes 25165832 | tf_op jit(solution)/shard_map/ppermute | solution.py:99
  72.3 55.7 %collective-permute-start.2 = (bf16[600,1024]{1,0:T(8,128)(2,1)}, bf16[600,1024]{1,0:T(8,128)(2,1)}, u32[]{:S(2)}, u32[]{:S(2)}) collective-permute-start(bf16[600,1024]{1,0:T(8,128)(2,1)} %collective-permute-done.1), channel_id=1, source_target_pairs={{0,4},{4,8},{8,12},{12,14},{14,10},{10,6},{6,2},{2,0},{1,5},{5,9},... | collective-permute-start | bytes 3686408 | tf_op jit(solution)/shard_map/ppermute | solution.py:107
  74.2 55.7 %collective-permute-start.5 = (bf16[600,1024]{1,0:T(8,128)(2,1)S(1)}, bf16[600,1024]{1,0:T(8,128)(2,1)}, u32[]{:S(2)}, u32[]{:S(2)}) collective-permute-start(bf16[600,1024]{1,0:T(8,128)(2,1)S(1)} %collective-permute-done.4), channel_id=1, source_target_pairs={{0,2},{4,0},{8,4},{12,8},{14,12},{10,14},{6,10},{2,6},{1,3},{5,1},... | collective-permute-start | bytes 3686408 | tf_op jit(solution)/shard_map/ppermute | solution.py:112
  74.4 99.9 %collective-permute-start.7 = (bf16[256,4096]{1,0:T(8,128)(2,1)}, bf16[256,4096]{1,0:T(8,128)(2,1)}, u32[]{:S(2)}, u32[]{:S(2)}) collective-permute-start(bf16[256,4096]{1,0:T(8,128)(2,1)} %param.15), channel_id=1, source_target_pairs={{0,1},{1,0},{2,3},{3,2},{4,5},{5,4},{6,7},{7,6},{8,9},{9,8},{10,11... | collective-permute-start | bytes 6291464 | tf_op jit(solution)/shard_map/ppermute | solution.py:100
  103.5 10.6 %copy-start.9 = (s32[8]{0:T(128)S(1)}, s32[8]{0:T(128)}, u32[]{:S(2)}) copy-start(s32[8]{0:T(128)} %constant.157.clone) | copy-start | bytes 100
  103.5 18.5 %copy-start.4 = (s32[8]{0:T(128)S(1)}, s32[8]{0:T(128)}, u32[]{:S(2)}) copy-start(s32[8]{0:T(128)} %constant.158.clone) | copy-start | bytes 100
  103.5 24.1 %copy-start.7 = (s32[1,4]{1,0:T(1,128)S(1)}, s32[1,4]{1,0:T(1,128)}, u32[]{:S(2)}) copy-start(s32[1,4]{1,0:T(1,128)} %param.18) | copy-start | bytes 52
  103.5 24.4 %copy-start.8 = (s32[1,4]{1,0:T(1,128)S(1)}, s32[1,4]{1,0:T(1,128)}, u32[]{:S(2)}) copy-start(s32[1,4]{1,0:T(1,128)} %param.19) | copy-start | bytes 52
  113.7 114.2 %collective-permute-start.11 = (bf16[1024,4096]{1,0:T(8,128)(2,1)}, bf16[1024,4096]{1,0:T(8,128)(2,1)}, u32[]{:S(2)}, u32[]{:S(2)}) collective-permute-start(bf16[1024,4096]{1,0:T(8,128)(2,1)} %mul.270), channel_id=1, source_target_pairs={{0,1},{1,0},{2,3},{3,2},{4,5},{5,4},{6,7},{7,6},{8,9},{9,8},{10,11... | collective-permute-start | bytes 25165832 | tf_op jit(solution)/shard_map/ppermute | solution.py:101
  128.0 29.2 %collective-permute-start.3 = (bf16[600,1024]{1,0:T(8,128)(2,1)}, bf16[600,1024]{1,0:T(8,128)(2,1)S(1)}, u32[]{:S(2)}, u32[]{:S(2)}) collective-permute-start(bf16[600,1024]{1,0:T(8,128)(2,1)} %collective-permute-done.2), channel_id=1, source_target_pairs={{0,4},{4,8},{8,12},{12,14},{14,10},{10,6},{6,2},{2,0},{1,5},{5,9},... | collective-permute-start | bytes 3686408 | tf_op jit(solution)/shard_map/ppermute | solution.py:107
  129.9 1.6 copy-start.3
  129.9 29.1 %collective-permute-start.6 = (bf16[600,1024]{1,0:T(8,128)(2,1)}, bf16[600,1024]{1,0:T(8,128)(2,1)S(1)}, u32[]{:S(2)}, u32[]{:S(2)}) collective-permute-start(bf16[600,1024]{1,0:T(8,128)(2,1)} %collective-permute-done.5), channel_id=1, source_target_pairs={{0,2},{4,0},{8,4},{12,8},{14,12},{10,14},{6,10},{2,6},{1,3},{5,1},... | collective-permute-start | bytes 3686408 | tf_op jit(solution)/shard_map/ppermute | solution.py:112
  159.2 3.7 copy-start
  159.2 3.7 copy-start.5
  174.3 5.9 %copy-start.2 = (bf16[600,8192]{1,0:T(8,128)(2,1)S(1)}, bf16[600,8192]{1,0:T(8,128)(2,1)}, u32[]{:S(2)}) copy-start(bf16[600,8192]{1,0:T(8,128)(2,1)} %fusion.2) | copy-start | bytes 29491204
  184.0 6.4 %collective-permute-start.8 = (bf16[600,128]{0,1:T(8,128)(2,1)S(1)}, bf16[600,128]{0,1:T(8,128)(2,1)S(1)}, u32[]{:S(2)}, u32[]{:S(2)}) collective-permute-start(bf16[600,128]{0,1:T(8,128)(2,1)S(1)} %get-tuple-element.19), channel_id=1, source_target_pairs={{0,2},{2,6},{4,10},{6,14},{8,0},{10,4},{12,8},{14,12},{1,3},{3,7},... | collective-permute-start | bytes 460808 | tf_op jit(solution)/shard_map/ppermute | solution.py:137
  185.8 4.7 %collective-permute-start.9 = (bf16[600,128]{0,1:T(8,128)(2,1)S(1)}, bf16[600,128]{0,1:T(8,128)(2,1)S(1)}, u32[]{:S(2)}, u32[]{:S(2)}) collective-permute-start(bf16[600,128]{0,1:T(8,128)(2,1)S(1)} %get-tuple-element.20), channel_id=1, source_target_pairs={{0,0},{2,4},{4,8},{6,12},{8,2},{10,6},{12,10},{14,14},{1,1},{3,5},... | collective-permute-start | bytes 460808 | tf_op jit(solution)/shard_map/ppermute | solution.py:136
  254.9 111.0 %copy-start.1 = (f32[600,8192]{1,0:T(8,128)}, f32[600,8192]{1,0:T(8,128)S(1)}, u32[]{:S(2)}) copy-start(f32[600,8192]{1,0:T(8,128)S(1)} %maximum_select_fusion) | copy-start | bytes 58982404
  255.3 30.9 %collective-permute-start.12 = (bf16[600,1024]{1,0:T(8,128)(2,1)S(1)}, bf16[600,1024]{1,0:T(8,128)(2,1)S(1)}, u32[]{:S(2)}, u32[]{:S(2)}) collective-permute-start(bf16[600,1024]{1,0:T(8,128)(2,1)S(1)} %get-tuple-element.11), channel_id=1, source_target_pairs={{0,4},{4,8},{8,12},{12,14},{14,10},{10,6},{6,2},{2,0},{1,5},{5,9},... | collective-permute-start | bytes 3686408 | tf_op jit(solution)/shard_map/ppermute | solution.py:174
  286.7 26.7 %collective-permute-start.13 = (bf16[600,1024]{1,0:T(8,128)(2,1)S(1)}, bf16[600,1024]{1,0:T(8,128)(2,1)S(1)}, u32[]{:S(2)}, u32[]{:S(2)}) collective-permute-start(bf16[600,1024]{1,0:T(8,128)(2,1)S(1)} %add_convert_fusion.5), channel_id=1, source_target_pairs={{0,4},{4,8},{8,12},{12,14},{14,10},{10,6},{6,2},{2,0},{1,5},{5,9},... | collective-permute-start | bytes 3686408 | tf_op jit(solution)/shard_map/ppermute | solution.py:174
  288.7 26.4 %collective-permute-start.16 = (bf16[600,1024]{1,0:T(8,128)(2,1)S(1)}, bf16[600,1024]{1,0:T(8,128)(2,1)S(1)}, u32[]{:S(2)}, u32[]{:S(2)}) collective-permute-start(bf16[600,1024]{1,0:T(8,128)(2,1)S(1)} %get-tuple-element.12), channel_id=1, source_target_pairs={{0,2},{4,0},{8,4},{12,8},{14,12},{10,14},{6,10},{2,6},{1,3},{5,1},... | collective-permute-start | bytes 3686408 | tf_op jit(solution)/shard_map/ppermute | solution.py:181
  313.9 25.3 %collective-permute-start.14 = (bf16[600,1024]{1,0:T(8,128)(2,1)S(1)}, bf16[600,1024]{1,0:T(8,128)(2,1)S(1)}, u32[]{:S(2)}, u32[]{:S(2)}) collective-permute-start(bf16[600,1024]{1,0:T(8,128)(2,1)S(1)} %add_convert_fusion.4), channel_id=1, source_target_pairs={{0,4},{4,8},{8,12},{12,14},{14,10},{10,6},{6,2},{2,0},{1,5},{5,9},... | collective-permute-start | bytes 3686408 | tf_op jit(solution)/shard_map/ppermute | solution.py:174
  340.2 25.7 %collective-permute-start.17 = (bf16[600,1024]{1,0:T(8,128)(2,1)S(1)}, bf16[600,1024]{1,0:T(8,128)(2,1)S(1)}, u32[]{:S(2)}, u32[]{:S(2)}) collective-permute-start(bf16[600,1024]{1,0:T(8,128)(2,1)S(1)} %get-tuple-element.10), channel_id=1, source_target_pairs={{0,2},{4,0},{8,4},{12,8},{14,12},{10,14},{6,10},{2,6},{1,3},{5,1},... | collective-permute-start | bytes 3686408 | tf_op jit(solution)/shard_map/ppermute | solution.py:181
  341.7 27.5 %collective-permute-start.15 = (bf16[600,1024]{1,0:T(8,128)(2,1)S(1)}, bf16[600,1024]{1,0:T(8,128)(2,1)}, u32[]{:S(2)}, u32[]{:S(2)}) collective-permute-start(bf16[600,1024]{1,0:T(8,128)(2,1)S(1)} %get-tuple-element.9), channel_id=1, source_target_pairs={{0,4},{4,8},{8,12},{12,14},{14,10},{10,6},{6,2},{2,0},{1,5},{5,9},... | collective-permute-start | bytes 3686408 | tf_op jit(solution)/shard_map/ppermute | solution.py:174
  366.3 25.1 %collective-permute-start.18 = (bf16[600,1024]{1,0:T(8,128)(2,1)S(1)}, bf16[600,1024]{1,0:T(8,128)(2,1)}, u32[]{:S(2)}, u32[]{:S(2)}) collective-permute-start(bf16[600,1024]{1,0:T(8,128)(2,1)S(1)} %add_convert_fusion.1), channel_id=1, source_target_pairs={{0,2},{4,0},{8,4},{12,8},{14,12},{10,14},{6,10},{2,6},{1,3},{5,1},... | collective-permute-start | bytes 3686408 | tf_op jit(solution)/shard_map/ppermute | solution.py:181

commit v2 on v1

--- a/solution.py
+++ b/solution.py
@@ -64,15 +64,22 @@
     return [z * x_size + x for z, x in cycle]
 
 
+def fast_prune(weight, keep):
+    rows, cols = weight.shape
+    step_r, step_c = rows // keep.shape[0], cols // keep.shape[1]
+    mask = jnp.repeat(keep.astype(weight.dtype), step_c, axis=1)
+    return (weight.reshape(keep.shape[0], step_r, cols) * mask[:, None, :]).reshape(rows, cols)
+
+
 def make_fast(n, order):
     position_of = np.zeros(n, np.int32)
     for p, t in enumerate(order):
         position_of[t] = p
     order_arr = np.asarray(order, np.int32)
-    to_next = [(order[i], order[(i + 1) % n]) for i in range(n)]
-    to_prev = [(order[i], order[(i - 1) % n]) for i in range(n)]
-    n_cw = n // 2
-    n_ccw = (n - 1) // 2
+    both = ("tensor", "dp")
+    ring_pairs = [(order[i] * 2, order[(i + 1) % n] * 2) for i in range(n)] + [
+        (order[i] * 2 + 1, order[(i - 1) % n] * 2 + 1) for i in range(n)
+    ]
 
     def on_device(
         hidden,
@@ -89,52 +96,48 @@
         dp_rank = lax.axis_index("dp")
         pos = jnp.asarray(position_of)[tensor_rank]
         ring = jnp.asarray(order_arr)
+        sign = 1 - 2 * dp_rank
         total_rows, feat = hidden.shape
         head_local = query_weight.shape[1] // HD
-        half_rows = query_weight.shape[0]
-
-        query_mine = prune(query_weight, query_keep)
-        out_mine = prune(out_weight, out_keep)
+
         swap = [(0, 1), (1, 0)]
-        query_other = lax.ppermute(query_mine, "dp", swap)
-        kv_other = lax.ppermute(kv_weight, "dp", swap)
-        out_other = lax.ppermute(out_mine, "dp", swap)
+        first = dp_rank == 0
+
+        def full_over_dp(local, axis):
+            other = lax.ppermute(local, "dp", swap)
+            return jnp.where(
+                first,
+                jnp.concatenate([local, other], axis=axis),
+                jnp.concatenate([other, local], axis=axis),
+            )
+
+        query_full = fast_prune(full_over_dp(query_weight, 0), full_over_dp(query_keep, 0))
+        kv_full = full_over_dp(kv_weight, 1)
+        out_full = fast_prune(full_over_dp(out_weight, 1), full_over_dp(out_keep, 1))
 
         whole = jnp.zeros((total_rows, n * feat), hidden.dtype)
         whole = lax.dynamic_update_slice(whole, hidden, (0, tensor_rank * feat))
-        fwd = hidden
-        for s in range(n_cw):
-            fwd = lax.ppermute(fwd, "tensor", to_next)
-            src = ring[(pos - s - 1) % n]
-            whole = lax.dynamic_update_slice(whole, fwd, (0, src * feat))
-        bwd = hidden
-        for s in range(n_ccw):
-            bwd = lax.ppermute(bwd, "tensor", to_prev)
-            src = ring[(pos + s + 1) % n]
-            whole = lax.dynamic_update_slice(whole, bwd, (0, src * feat))
+        moving = hidden
+        for s in range(n - 1):
+            moving = lax.ppermute(moving, both, ring_pairs)
+            src = ring[(pos - sign * (s + 1)) % n]
+            whole = lax.dynamic_update_slice(whole, moving, (0, src * feat))
 
         rows_float = whole.astype(jnp.float32)
         mean_square = jnp.mean(rows_float * rows_float, axis=-1, keepdims=True)
         normed = (rows_float * lax.rsqrt(mean_square + 1e-05) * norm_gain).astype(jnp.bfloat16)
-        mine_cols = lax.dynamic_slice_in_dim(normed, dp_rank * half_rows, half_rows, axis=1)
-        other_cols = lax.dynamic_slice_in_dim(normed, (1 - dp_rank) * half_rows, half_rows, axis=1)
-
-        queries_raw = jnp.dot(mine_cols, query_mine, preferred_element_type=jnp.float32) + jnp.dot(
-            other_cols, query_other, preferred_element_type=jnp.float32
-        )
-        contract = (((1,), (1,)), ((), ()))
-        kv_piece = (
-            lax.dot_general(mine_cols, kv_weight, contract, preferred_element_type=jnp.float32)
-            + lax.dot_general(other_cols, kv_other, contract, preferred_element_type=jnp.float32)
+        queries_raw = jnp.dot(normed, query_full, preferred_element_type=jnp.float32)
+        kv_piece = lax.dot_general(
+            normed, kv_full, (((1,), (1,)), ((), ())), preferred_element_type=jnp.float32
         ).astype(jnp.bfloat16)
 
         low = tensor_rank < n // 2
-        first = kv_piece[:, :HD]
-        second = kv_piece[:, HD:]
+        lo_cols = kv_piece[:, :HD]
+        hi_cols = kv_piece[:, HD:]
         pairs_a = [(s, 2 * s) if s < n // 2 else (s, 2 * (s - n // 2) + 1) for s in range(n)]
         pairs_b = [(s, 2 * s + 1) if s < n // 2 else (s, 2 * (s - n // 2)) for s in range(n)]
-        got_a = lax.ppermute(jnp.where(low, first, second), "tensor", pairs_a)
-        got_b = lax.ppermute(jnp.where(low, second, first), "tensor", pairs_b)
+        got_a = lax.ppermute(jnp.where(low, lo_cols, hi_cols), "tensor", pairs_a)
+        got_b = lax.ppermute(jnp.where(low, hi_cols, lo_cols), "tensor", pairs_b)
         even = tensor_rank % 2 == 0
         key_head = jnp.where(even, got_a, got_b)
         value_head = jnp.where(even, got_b, got_a)
@@ -155,30 +158,16 @@
         ).astype(jnp.bfloat16)
         context = context.reshape(total_rows, head_local * HD)
 
-        terms_mine = jnp.dot(context, out_mine, preferred_element_type=jnp.float32)
-        terms_other = jnp.dot(context, out_other, preferred_element_type=jnp.float32)
-        terms = jnp.where(
-            dp_rank == 0,
-            jnp.concatenate([terms_mine, terms_other], axis=1),
-            jnp.concatenate([terms_other, terms_mine], axis=1),
-        )
-
         def chunk(dest_pos):
-            return lax.dynamic_slice_in_dim(terms, ring[dest_pos % n] * feat, feat, axis=1)
-
+            cols = lax.dynamic_slice_in_dim(out_full, ring[dest_pos % n] * feat, feat, axis=1)
+            return jnp.dot(context, cols, preferred_element_type=jnp.float32)
+
+        acc = None
+        for s in range(n - 1):
+            part = chunk(pos + sign * (n - 1 - s))
+            send = part if acc is None else part + acc.astype(jnp.float32)
+            acc = lax.ppermute(send.astype(jnp.bfloat16), both, ring_pairs)
         total = chunk(pos)
-        acc = None
-        for s in range(n_cw):
-            part = chunk(pos + n_cw - s)
-            send = part if acc is None else part + acc.astype(jnp.float32)
-            acc = lax.ppermute(send.astype(jnp.bfloat16), "tensor", to_next)
-        if acc is not None:
-            total = total + acc.astype(jnp.float32)
-        acc = None
-        for s in range(n_ccw):
-            part = chunk(pos - (n_ccw - s))
-            send = part if acc is None else part + acc.astype(jnp.float32)
-            acc = lax.ppermute(send.astype(jnp.bfloat16), "tensor", to_prev)
         if acc is not None:
             total = total + acc.astype(jnp.float32)
         return total.astype(jnp.bfloat16)

time: 402 us -> 386 us (0.960); the launches traced: 396 us -> 385 us
  local copies, waits for them, and re-layouts: 69.6 us -> 47 us
  other arithmetic: 60.8 us -> 50.3 us
  between operations: 13.6 us -> 20.6 us
  waiting for transfers between devices: 171 us -> 178 us
  matrix products: 54.3 us -> 59.4 us
    mul x4 -> x2, local copies, waits for them, and re-layouts: 57.8 us -> 0.6 us  [fast_prune(): weight.reshape(keep.shape[0], step_r, cols) * mask[:, None, :]]
    dot_general x0 -> x1, local copies, waits for them, and re-layouts: none -> 21 us  [on_device(): jnp.dot(normed, query_full, preferred_element_type=jnp.float32)]
    dot_general x0 -> x1, other arithmetic: none -> 19.5 us  [on_device(): jnp.dot(normed, query_full, preferred_element_type=jnp.float32)]
    convert_element_type x8 -> x2, other arithmetic: 18.5 us -> 0.16 us  [fast_prune(): mask = jnp.repeat(keep.astype(weight.dtype), step_c, axis=1)]
    select_n x2 -> x1, other arithmetic: 16 us -> 0.04 us  [on_device(): got_b = lax.ppermute(jnp.where(low, hi_cols, lo_cols), 'tensor', pairs_b)]
    dynamic_update_slice x7, local copies, waits for them, and re-layouts: 4.87 us -> 13.2 us  [on_device(): whole = lax.dynamic_update_slice(whole, moving, (0, src * feat))]
    ppermute x19 -> x21, waiting for transfers between devices: 171 us -> 178 us  [the longest x7 105 us: on_device(): acc = lax.ppermute(send.astype(jnp.bfloat16), both, ring_pairs)]
    dot_general x6 -> x10, matrix products: 46.8 us -> 51.8 us  [the longest x8 28.3 us: chunk(): return jnp.dot(context, cols, preferred_element_type=jnp.float32)]
  transfers between devices with their start and end apart: 19 -> 21, of which waited for: 9 -> 14; matrix products, arithmetic and copies ran while one was open for 38% -> 28% of each run, Pallas kernels for 0% -> 0%
where the time goes in v2:
time: 386 us; the launch traced here: 385 us
  waiting for transfers between devices  178 us (46%)
  matrix products  59.4 us (15%)
  other arithmetic  50.3 us (13%)
  local copies, waits for them, and re-layouts  47 us (12%)
  starting transfers between devices  29.6 us (8%)
  between operations  20.6 us (5%)
    ppermute x7, waiting for transfers between devices, on_device(): acc = lax.ppermute(send.astype(jnp.bfloat16), both, ring_pairs)  105 us
    ppermute x7, waiting for transfers between devices, on_device(): moving = lax.ppermute(moving, both, ring_pairs)  72.1 us
    dot_general x8, matrix products, chunk(): return jnp.dot(context, cols, preferred_element_type=jnp.float32)  28.3 us
    dot_general x1, local copies, waits for them, and re-layouts, on_device(): jnp.dot(normed, query_full, preferred_element_type=jnp.float32)  21 us
    mul x1, other arithmetic, fast_prune(): weight.reshape(keep.shape[0], step_r, cols) * mask[:, None, :]  19.8 us
    dot_general x1, other arithmetic, on_device(): jnp.dot(normed, query_full, preferred_element_type=jnp.float32)  19.5 us
    ppermute x7, starting transfers between devices, on_device(): moving = lax.ppermute(moving, both, ring_pairs)  15.7 us
    dot_general x1, matrix products, on_device(): jnp.dot(normed, query_full, preferred_element_type=jnp.float32)  14.3 us
  transfers between devices with their start and end apart: 21, of which 14 were waited for; matrix products, arithmetic and copies ran while one was open for 28% of the time, Pallas kernels for 0%

profile of v2, /device:TPU:0, one launch (start us, length us, event | category | flops | bytes accessed | tf_op | source)
XLA Modules:
  0.0 385.2 jit_solution(2002931372909106516)
XLA Ops:
  0.0 3.1 collective-permute-start
  3.6 14.3 %collective-permute-done = bf16[600,1024]{1,0:T(8,128)(2,1)S(1)} collective-permute-done((bf16[600,1024]{1,0:T(8,128)(2,1)}, bf16[600,1024]{1,0:T(8,128)(2,1)S(1)}, u32[]{:S(2)}, u32[]{:S(2)}) %collective-permute-start) | collective-permute-done | bytes 1228832 | tf_op jit(solution)/shard_map/ppermute | solution.py:122
  17.9 2.1 collective-permute-start.1
  20.0 14.6 %collective-permute-done.1 = bf16[600,1024]{1,0:T(8,128)(2,1)S(1)} collective-permute-done((bf16[600,1024]{1,0:T(8,128)(2,1)S(1)}, bf16[600,1024]{1,0:T(8,128)(2,1)S(1)}, u32[]{:S(2)}, u32[]{:S(2)}) %collective-permute-start.1) | collective-permute-done | bytes 1228832 | tf_op jit(solution)/shard_map/ppermute | solution.py:122
  34.6 1.0 copy-done.1
  35.6 2.1 collective-permute-start.2
  37.8 14.6 %collective-permute-done.2 = bf16[600,1024]{1,0:T(8,128)(2,1)S(1)} collective-permute-done((bf16[600,1024]{1,0:T(8,128)(2,1)S(1)}, bf16[600,1024]{1,0:T(8,128)(2,1)S(1)}, u32[]{:S(2)}, u32[]{:S(2)}) %collective-permute-start.2) | collective-permute-done | bytes 1228832 | tf_op jit(solution)/shard_map/ppermute | solution.py:122
  52.4 1.0 copy-done.3
  53.4 2.1 collective-permute-start.3
  55.5 14.7 %collective-permute-done.3 = bf16[600,1024]{1,0:T(8,128)(2,1)} collective-permute-done((bf16[600,1024]{1,0:T(8,128)(2,1)S(1)}, bf16[600,1024]{1,0:T(8,128)(2,1)}, u32[]{:S(2)}, u32[]{:S(2)}) %collective-permute-start.3) | collective-permute-done | bytes 1228832 | tf_op jit(solution)/shard_map/ppermute | solution.py:122
  70.2 2.1 collective-permute-start.4
  72.9 1.3 dynamic_slice.72
  85.1 0.8 reduce-window.4
  86.0 1.2 collective-permute-done.4
  87.3 2.1 collective-permute-start.5
  89.4 0.7 fusion.102
  90.6 1.1 multiply_cosine_fusion
  91.7 12.6 %collective-permute-done.5 = bf16[600,1024]{1,0:T(8,128)(2,1)} collective-permute-done((bf16[600,1024]{1,0:T(8,128)(2,1)}, bf16[600,1024]{1,0:T(8,128)(2,1)}, u32[]{:S(2)}, u32[]{:S(2)}) %collective-permute-start.5) | collective-permute-done | bytes 1228832 | tf_op jit(solution)/shard_map/ppermute | solution.py:122
  104.3 2.1 collective-permute-start.6
  106.4 4.9 %broadcast_in_dim.19 = bf16[600,8192]{1,0:T(8,128)(2,1)} broadcast(bf16[]{:T(256)} %constant.132.clone.1), dimensions={} | broadcast | bytes 9830402 | tf_op jit(solution)/shard_map/broadcast_in_dim | solution.py:118
  111.4 1.2 constant_dynamic-update-slice_fusion.7
  112.6 0.7 fusion.109
  118.7 0.9 collective-permute-done.13
  120.5 1.2 constant_dynamic-update-slice_fusion.6
  122.2 1.2 constant_dynamic-update-slice_fusion.5
  123.3 1.2 constant_dynamic-update-slice_fusion.4
  124.5 2.4 constant_dynamic-update-slice_fusion.3
  126.9 2.4 constant_dynamic-update-slice_fusion.2
  129.3 2.5 constant_dynamic-update-slice_fusion.1
  131.8 19.5 %fusion.4 = bf16[1024,8192]{0,1:T(8,128)(2,1)} fusion(bf16[4096,1024]{1,0:T(8,128)(2,1)} %collective-permute-done.10, bf16[4096,1024]{1,0:T(8,128)(2,1)} %param.13, pred[]{:T(512)S(6)} %eq.54, bf16[128,1024]{1,0:T(8,128)(2,1)S(1)} %copy.24), kind=kLoop, calls=%fused_computation.7 | loop fusion | flops 109051904 | bytes 33816576 | tf_op jit(solution)/shard_map/dot_general | solution.py:129
  151.4 21.0 %copy.36 = bf16[1024,8192]{1,0:T(8,128)(2,1)} copy(bf16[1024,8192]{0,1:T(8,128)(2,1)} %fusion.4) | data formatting | bytes 33554432 | tf_op jit(solution)/shard_map/dot_general | solution.py:129
  172.4 19.8 %fusion.5 = bf16[1024,8192]{1,0:T(8,128)(2,1)} fusion(bf16[1024,4096]{1,0:T(8,128)(2,1)} %collective-permute-done.12, bf16[1024,4096]{1,0:T(8,128)(2,1)} %param.16, pred[]{:T(512)S(6)} %eq.54, bf16[16,8192]{1,0:T(8,128)(2,1)S(1)} %mul.329), kind=kLoop, calls=%fused_computation.9 | loop fusion | flops 109051904 | bytes 33816576 | tf_op jit(solution)/shard_map/mul | solution.py:71
  192.2 2.4 constant_dynamic-update-slice_fusion
  194.6 5.9 %fusion = f32[600]{0:T(1024)S(1)} fusion(bf16[600,8192]{1,0:T(8,128)(2,1)} %constant_dynamic-update-slice_fusion), kind=kLoop, calls=%fused_computation.2 | loop fusion | flops 14745000 | bytes 9832800 | tf_op jit(solution)/shard_map/reduce_sum | solution.py:127
  200.6 9.2 %fusion.66 = bf16[600,256]{0,1:T(8,128)(2,1)S(1)} fusion(bf16[256,4096]{1,0:T(8,128)(2,1)} %collective-permute-done.7, bf16[256,4096]{1,0:T(8,128)(2,1)S(1)} %copy-done.8, pred[]{:T(512)S(6)} %eq.54, bf16[600,8192]{1,0:T(8,128)(2,1)} %constant_dynamic-update-slice_fusion, f32[8192]{0:T(1024)S(1)} %copy-done.9, f32[600]{0:T(1024)S(1)} %add_rsqrt_fusion), kind=kOutput, calls=%fused_computation.65 | convolution fusion | flops 2555271168 | bytes 14367073 | tf_op jit(solution)/shard_map/dot_general | solution.py:130
  209.9 0.9 collective-permute-start.9
  210.8 14.3 %fusion.7 = f32[600,8,128]{2,0,1:T(8,128)S(1)} fusion(bf16[8,128,8192]{2,1,0:T(8,128)(2,1)} %bitcast.82, bf16[600,8192]{1,0:T(8,128)(2,1)} %constant_dynamic-update-slice_fusion, f32[8192]{0:T(1024)S(1)} %copy-done.9, f32[600]{0:T(1024)S(1)} %add_rsqrt_fusion), kind=kOutput, calls=%fused_computation.13 | convolution fusion | flops 10085990400 | bytes 29100384 | tf_op jit(solution)/shard_map/dot_general | solution.py:129
  225.2 0.9 subtract_convert_fusion
  226.1 0.7 fusion.82
  226.8 3.9 %fusion.6 = (f32[8,600]{1,0:T(8,128)S(1)}, f32[600,600,8]{1,0,2:T(8,128)S(1)}) fusion(pred[600,600]{0,1:T(8,128)(4,1)S(1)} %or_and_fusion, bf16[600,8,64]{2,0,1:T(8,128)(2,1)S(1)} %get-tuple-element.10, bf16[600,8,64]{2,0,1:T(8,128)(2,1)S(1)} %get-tuple-element.9, bf16[600,1,64]{0,2,1:T(8,128)(2,1)S(1)} %get-tuple-element.12, ...), kind=kOutput, calls=%fused_computation.12 | convolution fusion | flops 748680000 | bytes 13281600 | tf_op jit(solution)/shard_map/qhd,kd->hqk/dot_general | solution.py:153
  230.7 3.7 fusion.53
  234.4 1.1 copy-done.10
  235.5 3.0 fusion.35
  238.5 4.8 %collective-permute-start.14 = (bf16[600,1024]{1,0:T(8,128)(2,1)S(1)}, bf16[600,1024]{1,0:T(8,128)(2,1)S(1)}, u32[]{:S(2)}, u32[]{:S(2)}) collective-permute-start(bf16[600,1024]{1,0:T(8,128)(2,1)S(1)} %fusion.35), channel_id=1, source_target_pairs={{0,4},{4,8},{8,12},{12,14},{14,10},{10,6},{6,2},{2,0},{1,3},{5,1},... | collective-permute-start | bytes 3686408 | tf_op jit(solution)/shard_map/ppermute | solution.py:169
  243.8 15.1 %collective-permute-done.14 = bf16[600,1024]{1,0:T(8,128)(2,1)S(1)} collective-permute-done((bf16[600,1024]{1,0:T(8,128)(2,1)S(1)}, bf16[600,1024]{1,0:T(8,128)(2,1)S(1)}, u32[]{:S(2)}, u32[]{:S(2)}) %collective-permute-start.14) | collective-permute-done | bytes 1228832 | tf_op jit(solution)/shard_map/ppermute | solution.py:169
  258.9 3.4 add_convert_fusion.6
  262.3 1.4 collective-permute-start.15
  264.3 15.1 %collective-permute-done.15 = bf16[600,1024]{1,0:T(8,128)(2,1)S(1)} collective-permute-done((bf16[600,1024]{1,0:T(8,128)(2,1)S(1)}, bf16[600,1024]{1,0:T(8,128)(2,1)S(1)}, u32[]{:S(2)}, u32[]{:S(2)}) %collective-permute-start.15) | collective-permute-done | bytes 1228832 | tf_op jit(solution)/shard_map/ppermute | solution.py:169
  279.4 3.4 add_convert_fusion.5
  282.8 1.1 collective-permute-start.16
  284.6 15.0 %collective-permute-done.16 = bf16[600,1024]{1,0:T(8,128)(2,1)S(1)} collective-permute-done((bf16[600,1024]{1,0:T(8,128)(2,1)S(1)}, bf16[600,1024]{1,0:T(8,128)(2,1)S(1)}, u32[]{:S(2)}, u32[]{:S(2)}) %collective-permute-start.16) | collective-permute-done | bytes 1228832 | tf_op jit(solution)/shard_map/ppermute | solution.py:169
  299.6 3.4 add_convert_fusion.4
  303.0 1.1 collective-permute-start.17
  304.8 14.9 %collective-permute-done.17 = bf16[600,1024]{1,0:T(8,128)(2,1)S(1)} collective-permute-done((bf16[600,1024]{1,0:T(8,128)(2,1)S(1)}, bf16[600,1024]{1,0:T(8,128)(2,1)S(1)}, u32[]{:S(2)}, u32[]{:S(2)}) %collective-permute-start.17) | collective-permute-done | bytes 1228832 | tf_op jit(solution)/shard_map/ppermute | solution.py:169
  319.8 3.4 add_convert_fusion.3
  323.2 1.1 collective-permute-start.18
  324.9 15.1 %collective-permute-done.18 = bf16[600,1024]{1,0:T(8,128)(2,1)S(1)} collective-permute-done((bf16[600,1024]{1,0:T(8,128)(2,1)S(1)}, bf16[600,1024]{1,0:T(8,128)(2,1)S(1)}, u32[]{:S(2)}, u32[]{:S(2)}) %collective-permute-start.18) | collective-permute-done | bytes 1228832 | tf_op jit(solution)/shard_map/ppermute | solution.py:169
  340.0 3.4 add_convert_fusion.2
  343.4 1.1 collective-permute-start.19
  345.1 15.2 %collective-permute-done.19 = bf16[600,1024]{1,0:T(8,128)(2,1)} collective-permute-done((bf16[600,1024]{1,0:T(8,128)(2,1)S(1)}, bf16[600,1024]{1,0:T(8,128)(2,1)}, u32[]{:S(2)}, u32[]{:S(2)}) %collective-permute-start.19) | collective-permute-done | bytes 1228832 | tf_op jit(solution)/shard_map/ppermute | solution.py:169
  360.3 3.7 add_convert_fusion.1
  364.0 1.1 collective-permute-start.20
  365.8 15.0 %collective-permute-done.20 = bf16[600,1024]{1,0:T(8,128)(2,1)S(1)} collective-permute-done((bf16[600,1024]{1,0:T(8,128)(2,1)S(1)}, bf16[600,1024]{1,0:T(8,128)(2,1)S(1)}, u32[]{:S(2)}, u32[]{:S(2)}) %collective-permute-start.20) | collective-permute-done | bytes 1228832 | tf_op jit(solution)/shard_map/ppermute | solution.py:169
  380.8 4.4 %add_convert_fusion = bf16[600,1024]{1,0:T(8,128)(2,1)} fusion(bf16[600,1024]{1,0:T(8,128)(2,1)S(1)} %collective-permute-done.20, bf16[1024,8192]{1,0:T(8,128)(2,1)} %fusion.5, s32[]{:T(128)S(6)} %select_n.276, bf16[8,75,8,128]{3,2,1,0:T(8,128)(2,1)} %copy-done.10), kind=kOutput, calls=%fused_computation.24 | convolution fusion | flops 1260134400 | bytes 5783556 | tf_op jit(solution)/shard_map/dot_general | solution.py:163
  (47 shorter events, 3.5 us)
Async XLA Ops:
  0.0 17.9 %collective-permute-start = (bf16[600,1024]{1,0:T(8,128)(2,1)}, bf16[600,1024]{1,0:T(8,128)(2,1)S(1)}, u32[]{:S(2)}, u32[]{:S(2)}) collective-permute-start(bf16[600,1024]{1,0:T(8,128)(2,1)} %param.11), channel_id=1, source_target_pairs={{0,4},{4,8},{8,12},{12,14},{14,10},{10,6},{6,2},{2,0},{1,3},{5,1},... | collective-permute-start | bytes 3686408 | tf_op jit(solution)/shard_map/ppermute | solution.py:122
  3.1 128.8 %collective-permute-start.10 = (bf16[4096,1024]{1,0:T(8,128)(2,1)}, bf16[4096,1024]{1,0:T(8,128)(2,1)}, u32[]{:S(2)}, u32[]{:S(2)}) collective-permute-start(bf16[4096,1024]{1,0:T(8,128)(2,1)} %param.13), channel_id=1, source_target_pairs={{0,1},{1,0},{2,3},{3,2},{4,5},{5,4},{6,7},{7,6},{8,9},{9,8},{10,11... | collective-permute-start | bytes 25165832 | tf_op jit(solution)/shard_map/ppermute | solution.py:107
  3.1 169.3 %collective-permute-start.12 = (bf16[1024,4096]{1,0:T(8,128)(2,1)}, bf16[1024,4096]{1,0:T(8,128)(2,1)}, u32[]{:S(2)}, u32[]{:S(2)}) collective-permute-start(bf16[1024,4096]{1,0:T(8,128)(2,1)} %param.16), channel_id=1, source_target_pairs={{0,1},{1,0},{2,3},{3,2},{4,5},{5,4},{6,7},{7,6},{8,9},{9,8},{10,11... | collective-permute-start | bytes 25165832 | tf_op jit(solution)/shard_map/ppermute | solution.py:107
  17.9 16.7 %collective-permute-start.1 = (bf16[600,1024]{1,0:T(8,128)(2,1)S(1)}, bf16[600,1024]{1,0:T(8,128)(2,1)S(1)}, u32[]{:S(2)}, u32[]{:S(2)}) collective-permute-start(bf16[600,1024]{1,0:T(8,128)(2,1)S(1)} %collective-permute-done), channel_id=1, source_target_pairs={{0,4},{4,8},{8,12},{12,14},{14,10},{10,6},{6,2},{2,0},{1,3},{5,1},... | collective-permute-start | bytes 3686408 | tf_op jit(solution)/shard_map/ppermute | solution.py:122
  34.6 1.0 copy-start.1
  35.6 16.7 %collective-permute-start.2 = (bf16[600,1024]{1,0:T(8,128)(2,1)S(1)}, bf16[600,1024]{1,0:T(8,128)(2,1)S(1)}, u32[]{:S(2)}, u32[]{:S(2)}) collective-permute-start(bf16[600,1024]{1,0:T(8,128)(2,1)S(1)} %collective-permute-done.1), channel_id=1, source_target_pairs={{0,4},{4,8},{8,12},{12,14},{14,10},{10,6},{6,2},{2,0},{1,3},{5,1},... | collective-permute-start | bytes 3686408 | tf_op jit(solution)/shard_map/ppermute | solution.py:122
  52.4 1.0 copy-start.3
  53.4 16.8 %collective-permute-start.3 = (bf16[600,1024]{1,0:T(8,128)(2,1)S(1)}, bf16[600,1024]{1,0:T(8,128)(2,1)}, u32[]{:S(2)}, u32[]{:S(2)}) collective-permute-start(bf16[600,1024]{1,0:T(8,128)(2,1)S(1)} %collective-permute-done.2), channel_id=1, source_target_pairs={{0,4},{4,8},{8,12},{12,14},{14,10},{10,6},{6,2},{2,0},{1,3},{5,1},... | collective-permute-start | bytes 3686408 | tf_op jit(solution)/shard_map/ppermute | solution.py:122
  70.2 17.0 %collective-permute-start.4 = (bf16[600,1024]{1,0:T(8,128)(2,1)}, bf16[600,1024]{1,0:T(8,128)(2,1)}, u32[]{:S(2)}, u32[]{:S(2)}) collective-permute-start(bf16[600,1024]{1,0:T(8,128)(2,1)} %collective-permute-done.3), channel_id=1, source_target_pairs={{0,4},{4,8},{8,12},{12,14},{14,10},{10,6},{6,2},{2,0},{1,3},{5,1},... | collective-permute-start | bytes 3686408 | tf_op jit(solution)/shard_map/ppermute | solution.py:122
  72.4 128.2 %collective-permute-start.7 = (bf16[256,4096]{1,0:T(8,128)(2,1)}, bf16[256,4096]{1,0:T(8,128)(2,1)}, u32[]{:S(2)}, u32[]{:S(2)}) collective-permute-start(bf16[256,4096]{1,0:T(8,128)(2,1)} %param.15), channel_id=1, source_target_pairs={{0,1},{1,0},{2,3},{3,2},{4,5},{5,4},{6,7},{7,6},{8,9},{9,8},{10,11... | collective-permute-start | bytes 6291464 | tf_op jit(solution)/shard_map/ppermute | solution.py:107
  72.4 46.0 %collective-permute-start.11 = (s32[64,16]{0,1:T(8,128)}, s32[64,16]{0,1:T(8,128)S(1)}, u32[]{:S(2)}, u32[]{:S(2)}) collective-permute-start(s32[64,16]{0,1:T(8,128)} %param.14), channel_id=1, source_target_pairs={{0,1},{1,0},{2,3},{3,2},{4,5},{5,4},{6,7},{7,6},{8,9},{9,8},{10,11... | collective-permute-start | bytes 12296 | tf_op jit(solution)/shard_map/ppermute | solution.py:107
  87.3 17.0 %collective-permute-start.5 = (bf16[600,1024]{1,0:T(8,128)(2,1)}, bf16[600,1024]{1,0:T(8,128)(2,1)}, u32[]{:S(2)}, u32[]{:S(2)}) collective-permute-start(bf16[600,1024]{1,0:T(8,128)(2,1)} %collective-permute-done.4), channel_id=1, source_target_pairs={{0,4},{4,8},{8,12},{12,14},{14,10},{10,6},{6,2},{2,0},{1,3},{5,1},... | collective-permute-start | bytes 3686408 | tf_op jit(solution)/shard_map/ppermute | solution.py:122
  91.7 19.7 %copy-start = (bf16[600,1024]{1,0:T(8,128)(2,1)S(1)}, bf16[600,1024]{1,0:T(8,128)(2,1)}, u32[]{:S(2)}) copy-start(bf16[600,1024]{1,0:T(8,128)(2,1)} %param.11) | copy-start | bytes 3686404
  104.3 87.8 %collective-permute-start.6 = (bf16[600,1024]{1,0:T(8,128)(2,1)}, bf16[600,1024]{1,0:T(8,128)(2,1)}, u32[]{:S(2)}, u32[]{:S(2)}) collective-permute-start(bf16[600,1024]{1,0:T(8,128)(2,1)} %collective-permute-done.5), channel_id=1, source_target_pairs={{0,4},{4,8},{8,12},{12,14},{14,10},{10,6},{6,2},{2,0},{1,3},{5,1},... | collective-permute-start | bytes 3686408 | tf_op jit(solution)/shard_map/ppermute | solution.py:122
  111.4 1.2 copy-start.5
  111.4 6.9 %copy-start.7 = (s32[16,64]{1,0:T(8,128)S(1)}, s32[16,64]{1,0:T(8,128)}, u32[]{:S(2)}) copy-start(s32[16,64]{1,0:T(8,128)} %param.17) | copy-start | bytes 12292
  111.4 7.0 %copy-start.6 = (s32[64,16]{0,1:T(8,128)S(1)}, s32[64,16]{0,1:T(8,128)}, u32[]{:S(2)}) copy-start(s32[64,16]{0,1:T(8,128)} %param.14) | copy-start | bytes 12292
  118.3 1.2 collective-permute-start.13
  120.5 1.7 copy-start.2
  120.5 2.9 copy-start.4
  194.6 6.0 %copy-start.8 = (bf16[256,4096]{1,0:T(8,128)(2,1)S(1)}, bf16[256,4096]{1,0:T(8,128)(2,1)}, u32[]{:S(2)}) copy-start(bf16[256,4096]{1,0:T(8,128)(2,1)} %param.15) | copy-start | bytes 6291460
  194.6 6.0 %copy-start.9 = (f32[8192]{0:T(1024)S(1)}, f32[8192]{0:T(1024)}, u32[]{:S(2)}) copy-start(f32[8192]{0:T(1024)} %param.12) | copy-start | bytes 98308
  209.8 16.2 %collective-permute-start.8 = (bf16[600,128]{0,1:T(8,128)(2,1)S(1)}, bf16[600,128]{0,1:T(8,128)(2,1)S(1)}, u32[]{:S(2)}, u32[]{:S(2)}) collective-permute-start(bf16[600,128]{0,1:T(8,128)(2,1)S(1)} %get-tuple-element.13), channel_id=1, source_target_pairs={{0,2},{2,6},{4,10},{6,14},{8,0},{10,4},{12,8},{14,12},{1,3},{3,7},... | collective-permute-start | bytes 460808 | tf_op jit(solution)/shard_map/ppermute | solution.py:140
  209.9 16.1 %collective-permute-start.9 = (bf16[600,128]{0,1:T(8,128)(2,1)S(1)}, bf16[600,128]{0,1:T(8,128)(2,1)S(1)}, u32[]{:S(2)}, u32[]{:S(2)}) collective-permute-start(bf16[600,128]{0,1:T(8,128)(2,1)S(1)} %get-tuple-element.14), channel_id=1, source_target_pairs={{0,0},{2,4},{4,8},{6,12},{8,2},{10,6},{12,10},{14,14},{1,1},{3,5},... | collective-permute-start | bytes 460808 | tf_op jit(solution)/shard_map/ppermute | solution.py:139
  234.4 1.1 copy-start.10
  238.5 20.4 %collective-permute-start.14 = (bf16[600,1024]{1,0:T(8,128)(2,1)S(1)}, bf16[600,1024]{1,0:T(8,128)(2,1)S(1)}, u32[]{:S(2)}, u32[]{:S(2)}) collective-permute-start(bf16[600,1024]{1,0:T(8,128)(2,1)S(1)} %fusion.35), channel_id=1, source_target_pairs={{0,4},{4,8},{8,12},{12,14},{14,10},{10,6},{6,2},{2,0},{1,3},{5,1},... | collective-permute-start | bytes 3686408 | tf_op jit(solution)/shard_map/ppermute | solution.py:169
  262.3 17.0 %collective-permute-start.15 = (bf16[600,1024]{1,0:T(8,128)(2,1)S(1)}, bf16[600,1024]{1,0:T(8,128)(2,1)S(1)}, u32[]{:S(2)}, u32[]{:S(2)}) collective-permute-start(bf16[600,1024]{1,0:T(8,128)(2,1)S(1)} %add_convert_fusion.6), channel_id=1, source_target_pairs={{0,4},{4,8},{8,12},{12,14},{14,10},{10,6},{6,2},{2,0},{1,3},{5,1},... | collective-permute-start | bytes 3686408 | tf_op jit(solution)/shard_map/ppermute | solution.py:169
  282.8 16.8 %collective-permute-start.16 = (bf16[600,1024]{1,0:T(8,128)(2,1)S(1)}, bf16[600,1024]{1,0:T(8,128)(2,1)S(1)}, u32[]{:S(2)}, u32[]{:S(2)}) collective-permute-start(bf16[600,1024]{1,0:T(8,128)(2,1)S(1)} %add_convert_fusion.5), channel_id=1, source_target_pairs={{0,4},{4,8},{8,12},{12,14},{14,10},{10,6},{6,2},{2,0},{1,3},{5,1},... | collective-permute-start | bytes 3686408 | tf_op jit(solution)/shard_map/ppermute | solution.py:169
  303.0 16.8 %collective-permute-start.17 = (bf16[600,1024]{1,0:T(8,128)(2,1)S(1)}, bf16[600,1024]{1,0:T(8,128)(2,1)S(1)}, u32[]{:S(2)}, u32[]{:S(2)}) collective-permute-start(bf16[600,1024]{1,0:T(8,128)(2,1)S(1)} %add_convert_fusion.4), channel_id=1, source_target_pairs={{0,4},{4,8},{8,12},{12,14},{14,10},{10,6},{6,2},{2,0},{1,3},{5,1},... | collective-permute-start | bytes 3686408 | tf_op jit(solution)/shard_map/ppermute | solution.py:169
  323.2 16.8 %collective-permute-start.18 = (bf16[600,1024]{1,0:T(8,128)(2,1)S(1)}, bf16[600,1024]{1,0:T(8,128)(2,1)S(1)}, u32[]{:S(2)}, u32[]{:S(2)}) collective-permute-start(bf16[600,1024]{1,0:T(8,128)(2,1)S(1)} %add_convert_fusion.3), channel_id=1, source_target_pairs={{0,4},{4,8},{8,12},{12,14},{14,10},{10,6},{6,2},{2,0},{1,3},{5,1},... | collective-permute-start | bytes 3686408 | tf_op jit(solution)/shard_map/ppermute | solution.py:169
  343.4 16.9 %collective-permute-start.19 = (bf16[600,1024]{1,0:T(8,128)(2,1)S(1)}, bf16[600,1024]{1,0:T(8,128)(2,1)}, u32[]{:S(2)}, u32[]{:S(2)}) collective-permute-start(bf16[600,1024]{1,0:T(8,128)(2,1)S(1)} %add_convert_fusion.2), channel_id=1, source_target_pairs={{0,4},{4,8},{8,12},{12,14},{14,10},{10,6},{6,2},{2,0},{1,3},{5,1},... | collective-permute-start | bytes 3686408 | tf_op jit(solution)/shard_map/ppermute | solution.py:169
  364.0 16.8 %collective-permute-start.20 = (bf16[600,1024]{1,0:T(8,128)(2,1)S(1)}, bf16[600,1024]{1,0:T(8,128)(2,1)S(1)}, u32[]{:S(2)}, u32[]{:S(2)}) collective-permute-start(bf16[600,1024]{1,0:T(8,128)(2,1)S(1)} %add_convert_fusion.1), channel_id=1, source_target_pairs={{0,4},{4,8},{8,12},{12,14},{14,10},{10,6},{6,2},{2,0},{1,3},{5,1},... | collective-permute-start | bytes 3686408 | tf_op jit(solution)/shard_map/ppermute | solution.py:169

commit v3 on v2

--- a/solution.py
+++ b/solution.py
@@ -100,20 +100,9 @@
         total_rows, feat = hidden.shape
         head_local = query_weight.shape[1] // HD
 
-        swap = [(0, 1), (1, 0)]
-        first = dp_rank == 0
-
-        def full_over_dp(local, axis):
-            other = lax.ppermute(local, "dp", swap)
-            return jnp.where(
-                first,
-                jnp.concatenate([local, other], axis=axis),
-                jnp.concatenate([other, local], axis=axis),
-            )
-
-        query_full = fast_prune(full_over_dp(query_weight, 0), full_over_dp(query_keep, 0))
-        kv_full = full_over_dp(kv_weight, 1)
-        out_full = fast_prune(full_over_dp(out_weight, 1), full_over_dp(out_keep, 1))
+        query_full = lax.all_gather(fast_prune(query_weight, query_keep), "dp", axis=0, tiled=True)
+        kv_full = lax.all_gather(kv_weight, "dp", axis=1, tiled=True)
+        out_full = lax.all_gather(fast_prune(out_weight, out_keep), "dp", axis=1, tiled=True)
 
         whole = jnp.zeros((total_rows, n * feat), hidden.dtype)
         whole = lax.dynamic_update_slice(whole, hidden, (0, tensor_rank * feat))
@@ -162,12 +151,13 @@
             cols = lax.dynamic_slice_in_dim(out_full, ring[dest_pos % n] * feat, feat, axis=1)
             return jnp.dot(context, cols, preferred_element_type=jnp.float32)
 
+        parts = [chunk(pos + sign * (n - 1 - s)) for s in range(n)]
+        parts = [parts[0].astype(jnp.bfloat16)] + lax.optimization_barrier(parts[1:])
         acc = None
         for s in range(n - 1):
-            part = chunk(pos + sign * (n - 1 - s))
-            send = part if acc is None else part + acc.astype(jnp.float32)
-            acc = lax.ppermute(send.astype(jnp.bfloat16), both, ring_pairs)
-        total = chunk(pos)
+            send = parts[0] if acc is None else (parts[s] + acc.astype(jnp.float32)).astype(jnp.bfloat16)
+            acc = lax.ppermute(send, both, ring_pairs)
+        total = parts[n - 1]
         if acc is not None:
             total = total + acc.astype(jnp.float32)
         return total.astype(jnp.bfloat16)

time: 386 us -> 331 us (0.86)
  local copies, waits for them, and re-layouts: 47 us -> 15.2 us
  other arithmetic: 50.3 us -> 28.7 us
  waiting for transfers between devices: 178 us -> 164 us
  between operations: 20.6 us -> 34.3 us
  matrix products: 59.4 us -> 50.6 us
  starting transfers between devices: 29.6 us -> 34.3 us
    dot_general x1 -> x0, local copies, waits for them, and re-layouts: 21 us -> none  [on_device(): jnp.dot(normed, query_full, preferred_element_type=jnp.float32)]
    dot_general x1 -> x0, other arithmetic: 19.5 us -> none  [on_device(): jnp.dot(normed, query_full, preferred_element_type=jnp.float32)]
    ppermute x12 -> x7, waiting for transfers between devices: 106 us -> 88.5 us  [on_device(): acc = lax.ppermute(send, both, ring_pairs)]
    dot_general x8, matrix products: 28.3 us -> 17.2 us  [chunk(): return jnp.dot(context, cols, preferred_element_type=jnp.float32)]
    dynamic_update_slice x7, local copies, waits for them, and re-layouts: 13.2 us -> 4.99 us  [on_device(): whole = lax.dynamic_update_slice(whole, moving, (0, src * feat))]
    ppermute x1, waiting for transfers between devices: 0.01 us -> 5.15 us  [on_device(): got_b = lax.ppermute(jnp.where(low, hi_cols, lo_cols), 'tensor', pairs_b)]
    ppermute x12 -> x7, starting transfers between devices: 13 us -> 18 us  [on_device(): acc = lax.ppermute(send, both, ring_pairs)]
    convert_element_type x0 -> x7, other arithmetic: none -> 4.17 us  [the longest x6 2.68 us: on_device(): (parts[s] + acc.astype(jnp.float32)).astype(jnp.bfloat16)]
  transfers between devices with their start and end apart: 21 -> 19, of which waited for: 14 -> 14; matrix products, arithmetic and copies ran while one was open for 28% -> 25% of each run, Pallas kernels for 0% -> 0%
where the time goes in v3:
time: 331 us; the launch traced here: 327 us
  waiting for transfers between devices  164 us (50%)
  matrix products  50.6 us (15%)
  starting transfers between devices  34.3 us (10%)
  between operations  34.3 us (10%)
  other arithmetic  28.7 us (9%)
  local copies, waits for them, and re-layouts  15.2 us (5%)
    ppermute x7, waiting for transfers between devices, on_device(): acc = lax.ppermute(send, both, ring_pairs)  88.5 us
    ppermute x7, waiting for transfers between devices, on_device(): moving = lax.ppermute(moving, both, ring_pairs)  69.8 us
    mul x2, other arithmetic, fast_prune(): weight.reshape(keep.shape[0], step_r, cols) * mask[:, None, :]  18.3 us
    ppermute x7, starting transfers between devices, on_device(): acc = lax.ppermute(send, both, ring_pairs)  18 us
    dot_general x8, matrix products, chunk(): return jnp.dot(context, cols, preferred_element_type=jnp.float32)  17.2 us
    dot_general x1, matrix products, on_device(): jnp.dot(normed, query_full, preferred_element_type=jnp.float32)  15.8 us
    ppermute x7, starting transfers between devices, on_device(): moving = lax.ppermute(moving, both, ring_pairs)  15.5 us
    dot_general x1, matrix products, on_device(): lax.dot_general(normed, kv_full, (((1,), (1,)), ((), ())), preferred_elem...  8.69 us
  transfers between devices with their start and end apart: 19, of which 14 were waited for; matrix products, arithmetic and copies ran while one was open for 25% of the time, Pallas kernels for 0%

profile of v3, /device:TPU:0, one launch (start us, length us, event | category | flops | bytes accessed | tf_op | source)
XLA Modules:
  0.0 327.4 jit_solution(2374955469329896723)
XLA Ops:
  6.5 0.7 all-gather.4.cloned.1.call-update
  7.3 0.7 convert_element_type.92
  8.5 7.3 %bitcast_multiply_fusion.1 = bf16[4096,1024]{1,0:T(8,128)(2,1)} fusion(bf16[4096,1024]{1,0:T(8,128)(2,1)} %param.13, bf16[64,1024]{1,0:T(8,128)(2,1)S(1)} %mul.314), kind=kLoop, calls=%fused_computation.9 | loop fusion | flops 4194304 | bytes 16908288 | tf_op jit(solution)/shard_map/mul | solution.py:71
  15.9 1.2 copy-done.1
  17.1 3.2 collective-permute-start
  20.3 14.6 %collective-permute-done = bf16[600,1024]{1,0:T(8,128)(2,1)S(1)} collective-permute-done((bf16[600,1024]{1,0:T(8,128)(2,1)S(1)}, bf16[600,1024]{1,0:T(8,128)(2,1)S(1)}, u32[]{:S(2)}, u32[]{:S(2)}) %collective-permute-start) | collective-permute-done | bytes 1228832 | tf_op jit(solution)/shard_map/ppermute | solution.py:111
  34.9 2.1 collective-permute-start.1
  37.5 11.0 %bitcast_multiply_fusion = bf16[1024,4096]{1,0:T(8,128)(2,1)} fusion(bf16[1024,4096]{1,0:T(8,128)(2,1)} %param.16, bf16[16,4096]{1,0:T(8,128)(2,1)S(1)} %mul.329), kind=kLoop, calls=%fused_computation.8 | loop fusion | flops 4194304 | bytes 16908288 | tf_op jit(solution)/shard_map/mul | solution.py:71
  48.5 3.2 collective-permute-done.1
  51.8 2.1 collective-permute-start.2
  53.9 14.8 %collective-permute-done.2 = bf16[600,1024]{1,0:T(8,128)(2,1)S(1)} collective-permute-done((bf16[600,1024]{1,0:T(8,128)(2,1)}, bf16[600,1024]{1,0:T(8,128)(2,1)S(1)}, u32[]{:S(2)}, u32[]{:S(2)}) %collective-permute-start.2) | collective-permute-done | bytes 1228832 | tf_op jit(solution)/shard_map/ppermute | solution.py:111
  68.7 1.0 copy-done.2
  69.7 2.1 collective-permute-start.3
  71.8 14.6 %collective-permute-done.3 = bf16[600,1024]{1,0:T(8,128)(2,1)S(1)} collective-permute-done((bf16[600,1024]{1,0:T(8,128)(2,1)S(1)}, bf16[600,1024]{1,0:T(8,128)(2,1)S(1)}, u32[]{:S(2)}, u32[]{:S(2)}) %collective-permute-start.3) | collective-permute-done | bytes 1228832 | tf_op jit(solution)/shard_map/ppermute | solution.py:111
  86.5 1.0 copy-done.4
  87.5 2.1 collective-permute-start.4
  89.6 14.7 %collective-permute-done.4 = bf16[600,1024]{1,0:T(8,128)(2,1)} collective-permute-done((bf16[600,1024]{1,0:T(8,128)(2,1)S(1)}, bf16[600,1024]{1,0:T(8,128)(2,1)}, u32[]{:S(2)}, u32[]{:S(2)}) %collective-permute-start.4) | collective-permute-done | bytes 1228832 | tf_op jit(solution)/shard_map/ppermute | solution.py:111
  104.3 2.1 collective-permute-start.5
  106.4 0.6 dynamic_slice.72
  118.0 0.8 fusion.86
  128.6 1.8 collective-permute-start.6
  130.4 1.2 broadcast_in_dim.19
  131.7 1.1 multiply_cosine_fusion
  133.1 1.6 constant_dynamic-update-slice_fusion.5
  135.1 1.4 constant_dynamic-update-slice_fusion.2
  136.5 1.4 constant_dynamic-update-slice_fusion.1
  138.0 7.8 %collective-permute-done.6 = bf16[600,1024]{1,0:T(8,128)(2,1)S(1)} collective-permute-done((bf16[600,1024]{1,0:T(8,128)(2,1)}, bf16[600,1024]{1,0:T(8,128)(2,1)S(1)}, u32[]{:S(2)}, u32[]{:S(2)}) %collective-permute-start.6) | collective-permute-done | bytes 1228832 | tf_op jit(solution)/shard_map/ppermute | solution.py:111
  145.9 2.0 fusion
  147.9 1.7 copy-done
  149.7 8.7 %fusion.45 = bf16[600,256]{0,1:T(8,128)(2,1)S(1)} fusion(bf16[256,8192]{1,0:T(8,128)(2,1)} %all-gather.4.cloned.1.call-done, bf16[600,8192]{1,0:T(8,128)(2,1)} %copy-done, f32[8192]{0:T(1024)S(1)} %copy-done.11, f32[600]{0:T(1024)S(1)} %add_rsqrt_fusion), kind=kOutput, calls=%fused_computation.55 | convolution fusion | flops 2536396800 | bytes 14367072 | tf_op jit(solution)/shard_map/dot_general | solution.py:119
  158.5 0.7 collective-permute-start.8
  159.5 5.1 %collective-permute-done.7 = bf16[600,128]{0,1:T(8,128)(2,1)S(1)} collective-permute-done((bf16[600,128]{0,1:T(8,128)(2,1)S(1)}, bf16[600,128]{0,1:T(8,128)(2,1)S(1)}, u32[]{:S(2)}, u32[]{:S(2)}) %collective-permute-start.7) | collective-permute-done | bytes 153632 | tf_op jit(solution)/shard_map/ppermute | solution.py:129
  164.7 0.7 fusion.61
  165.4 15.8 %fusion.25 = f32[75,8,8,128]{3,1,2,0:T(8,128)S(1)} fusion(bf16[8192,1024]{1,0:T(8,128)(2,1)} %all-gather.6.cloned.1.call-done, bf16[600,8192]{1,0:T(8,128)(2,1)} %copy-done, f32[8192]{0:T(1024)S(1)} %copy-done.11, f32[600]{0:T(1024)S(1)} %add_rsqrt_fusion), kind=kOutput, calls=%fused_computation.38 | convolution fusion | flops 10085990400 | bytes 29100384 | tf_op jit(solution)/shard_map/dot_general | solution.py:118
  181.2 0.6 copy.43
  181.8 0.8 fusion.85
  182.6 1.0 subtract_convert_fusion
  183.5 4.0 %fusion.3 = (f32[8,600]{1,0:T(8,128)S(1)}, f32[600,600,8]{1,0,2:T(8,128)S(1)}) fusion(pred[600,600]{0,1:T(8,128)(4,1)S(1)} %or_and_fusion, bf16[600,8,64]{2,0,1:T(8,128)(2,1)S(1)} %get-tuple-element.24, bf16[600,8,64]{2,0,1:T(8,128)(2,1)S(1)} %get-tuple-element.23, bf16[600,1,64]{0,2,1:T(8,128)(2,1)S(1)} %get-tuple-element.28, ...), kind=kOutput, calls=%fused_computation.7 | convolution fusion | flops 748680000 | bytes 13281600 | tf_op jit(solution)/shard_map/qhd,kd->hqk/dot_general | solution.py:142
  187.5 4.9 %fusion.32 = bf16[8,75,8,128]{3,2,1,0:T(8,128)(2,1)} fusion(f32[600,600,8]{1,0,2:T(8,128)S(1)} %get-tuple-element.51, f32[8,600]{1,0:T(8,128)S(1)} %get-tuple-element.50, pred[600,600]{0,1:T(8,128)(4,1)S(1)} %or_and_fusion, bf16[600,128]{0,1:T(8,128)(2,1)S(1)} %collective-permute-done.7, bf16[600,128]{0,1:T(8,128)(2,1)S(1)} %collective-permute-done.8, ...), kind=kOutput, calls=%fused_computation.42 | convolution fusion | flops 749491200 | bytes 13435201 | tf_op jit(solution)/shard_map/hqk,kd->qhd/dot_general | solution.py:145
  192.5 3.6 %fusion.28 = bf16[600,1024]{1,0:T(8,128)(2,1)S(1)} fusion(bf16[1024,8192]{1,0:T(8,128)(2,1)} %all-gather.8.cloned.1.call-done, s32[]{:T(128)S(6)} %select_n.243, bf16[8,75,8,128]{3,2,1,0:T(8,128)(2,1)} %fusion.32), kind=kOutput, calls=%fused_computation.39 | convolution fusion | flops 1258905600 | bytes 4554756 | tf_op jit(solution)/shard_map/dot_general | solution.py:152
  196.1 4.9 %collective-permute-start.9 = (bf16[600,1024]{1,0:T(8,128)(2,1)S(1)}, bf16[600,1024]{1,0:T(8,128)(2,1)S(1)}, u32[]{:S(2)}, u32[]{:S(2)}) collective-permute-start(bf16[600,1024]{1,0:T(8,128)(2,1)S(1)} %fusion.28), channel_id=1, source_target_pairs={{0,4},{4,8},{8,12},{12,14},{14,10},{10,6},{6,2},{2,0},{1,3},{5,1},... | collective-permute-start | bytes 3686408 | tf_op jit(solution)/shard_map/ppermute | solution.py:159
  201.0 3.4 %fusion.11 = f32[600,1024]{1,0:T(8,128)S(1)} fusion(bf16[1024,8192]{1,0:T(8,128)(2,1)} %all-gather.8.cloned.1.call-done, s32[]{:T(128)S(6)} %select_n.240, bf16[8,75,8,128]{3,2,1,0:T(8,128)(2,1)} %fusion.32), kind=kOutput, calls=%fused_computation.24 | convolution fusion | flops 1258291200 | bytes 5783556 | tf_op jit(solution)/shard_map/dot_general | solution.py:152
  204.4 2.9 fusion.13
  207.3 1.5 fusion.15
  208.7 1.5 fusion.17
  210.2 1.5 fusion.19
  211.7 1.5 fusion.21
  213.2 1.5 fusion.23
  214.7 0.9 collective-permute-done.9
  215.5 0.4 add_convert_fusion.6
  216.0 2.2 collective-permute-start.10
  218.2 14.6 %collective-permute-done.10 = bf16[600,1024]{1,0:T(8,128)(2,1)S(1)} collective-permute-done((bf16[600,1024]{1,0:T(8,128)(2,1)S(1)}, bf16[600,1024]{1,0:T(8,128)(2,1)S(1)}, u32[]{:S(2)}, u32[]{:S(2)}) %collective-permute-start.10) | collective-permute-done | bytes 1228832 | tf_op jit(solution)/shard_map/ppermute | solution.py:159
  232.8 0.4 add_convert_fusion.5
  233.2 2.2 collective-permute-start.11
  235.4 14.6 %collective-permute-done.11 = bf16[600,1024]{1,0:T(8,128)(2,1)S(1)} collective-permute-done((bf16[600,1024]{1,0:T(8,128)(2,1)S(1)}, bf16[600,1024]{1,0:T(8,128)(2,1)S(1)}, u32[]{:S(2)}, u32[]{:S(2)}) %collective-permute-start.11) | collective-permute-done | bytes 1228832 | tf_op jit(solution)/shard_map/ppermute | solution.py:159
  250.5 2.2 collective-permute-start.12
  252.7 14.6 %collective-permute-done.12 = bf16[600,1024]{1,0:T(8,128)(2,1)S(1)} collective-permute-done((bf16[600,1024]{1,0:T(8,128)(2,1)S(1)}, bf16[600,1024]{1,0:T(8,128)(2,1)S(1)}, u32[]{:S(2)}, u32[]{:S(2)}) %collective-permute-start.12) | collective-permute-done | bytes 1228832 | tf_op jit(solution)/shard_map/ppermute | solution.py:159
  267.7 2.2 collective-permute-start.13
  269.9 14.6 %collective-permute-done.13 = bf16[600,1024]{1,0:T(8,128)(2,1)S(1)} collective-permute-done((bf16[600,1024]{1,0:T(8,128)(2,1)S(1)}, bf16[600,1024]{1,0:T(8,128)(2,1)S(1)}, u32[]{:S(2)}, u32[]{:S(2)}) %collective-permute-start.13) | collective-permute-done | bytes 1228832 | tf_op jit(solution)/shard_map/ppermute | solution.py:159
  284.9 2.2 collective-permute-start.14
  287.1 14.6 %collective-permute-done.14 = bf16[600,1024]{1,0:T(8,128)(2,1)S(1)} collective-permute-done((bf16[600,1024]{1,0:T(8,128)(2,1)S(1)}, bf16[600,1024]{1,0:T(8,128)(2,1)S(1)}, u32[]{:S(2)}, u32[]{:S(2)}) %collective-permute-start.14) | collective-permute-done | bytes 1228832 | tf_op jit(solution)/shard_map/ppermute | solution.py:159
  302.2 2.2 collective-permute-start.15
  304.4 14.6 %collective-permute-done.15 = bf16[600,1024]{1,0:T(8,128)(2,1)S(1)} collective-permute-done((bf16[600,1024]{1,0:T(8,128)(2,1)S(1)}, bf16[600,1024]{1,0:T(8,128)(2,1)S(1)}, u32[]{:S(2)}, u32[]{:S(2)}) %collective-permute-start.15) | collective-permute-done | bytes 1228832 | tf_op jit(solution)/shard_map/ppermute | solution.py:159
  319.0 1.5 add_convert_fusion
  (61 shorter events, 4.7 us)
Async XLA Ops:
  6.5 143.1 %all-gather.4.cloned.1.call-start = ((), (), s32[]{:S(2)}) async-start(), calls=%async_computation | async-start | bytes 6291456 | tf_op jit(solution)/shard_map/all_gather | solution.py:104
  7.3 158.2 %all-gather.6.cloned.1.call-start = ((), (), s32[]{:S(2)}) async-start(), calls=%async_computation.1 | async-start | bytes 25165824 | tf_op jit(solution)/shard_map/all_gather | solution.py:103
  15.8 1.3 copy-start.1
  15.8 21.2 %copy-start.7 = (s32[16,64]{1,0:T(8,128)S(1)}, s32[16,64]{1,0:T(8,128)}, u32[]{:S(2)}) copy-start(s32[16,64]{1,0:T(8,128)} %param.17) | copy-start | bytes 12292
  15.8 176.7 %all-gather.8.cloned.1.call-start = ((), (), s32[]{:S(2)}) async-start(), calls=%async_computation.2 | async-start | bytes 25165824 | tf_op jit(solution)/shard_map/all_gather | solution.py:105
  17.1 17.8 %collective-permute-start = (bf16[600,1024]{1,0:T(8,128)(2,1)S(1)}, bf16[600,1024]{1,0:T(8,128)(2,1)S(1)}, u32[]{:S(2)}, u32[]{:S(2)}) collective-permute-start(bf16[600,1024]{1,0:T(8,128)(2,1)S(1)} %copy-done.1), channel_id=1, source_target_pairs={{0,4},{4,8},{8,12},{12,14},{14,10},{10,6},{6,2},{2,0},{1,3},{5,1},... | collective-permute-start | bytes 3686408 | tf_op jit(solution)/shard_map/ppermute | solution.py:111
  34.9 16.8 %collective-permute-start.1 = (bf16[600,1024]{1,0:T(8,128)(2,1)S(1)}, bf16[600,1024]{1,0:T(8,128)(2,1)}, u32[]{:S(2)}, u32[]{:S(2)}) collective-permute-start(bf16[600,1024]{1,0:T(8,128)(2,1)S(1)} %collective-permute-done), channel_id=1, source_target_pairs={{0,4},{4,8},{8,12},{12,14},{14,10},{10,6},{6,2},{2,0},{1,3},{5,1},... | collective-permute-start | bytes 3686408 | tf_op jit(solution)/shard_map/ppermute | solution.py:111
  48.5 57.9 %copy-start.12 = (s32[8]{0:T(128)S(1)}, s32[8]{0:T(128)}, u32[]{:S(2)}) copy-start(s32[8]{0:T(128)} %constant.148.clone) | copy-start | bytes 100
  48.5 69.5 %copy-start.6 = (s32[8]{0:T(128)S(1)}, s32[8]{0:T(128)}, u32[]{:S(2)}) copy-start(s32[8]{0:T(128)} %constant.149.clone) | copy-start | bytes 100
  48.5 79.6 %copy-start.8 = (s32[1,4]{1,0:T(1,128)S(1)}, s32[1,4]{1,0:T(1,128)}, u32[]{:S(2)}) copy-start(s32[1,4]{1,0:T(1,128)} %param.18) | copy-start | bytes 52
  48.5 79.9 %copy-start.9 = (s32[1,4]{1,0:T(1,128)S(1)}, s32[1,4]{1,0:T(1,128)}, u32[]{:S(2)}) copy-start(s32[1,4]{1,0:T(1,128)} %param.19) | copy-start | bytes 52
  51.8 16.9 %collective-permute-start.2 = (bf16[600,1024]{1,0:T(8,128)(2,1)}, bf16[600,1024]{1,0:T(8,128)(2,1)S(1)}, u32[]{:S(2)}, u32[]{:S(2)}) collective-permute-start(bf16[600,1024]{1,0:T(8,128)(2,1)} %collective-permute-done.1), channel_id=1, source_target_pairs={{0,4},{4,8},{8,12},{12,14},{14,10},{10,6},{6,2},{2,0},{1,3},{5,1},... | collective-permute-start | bytes 3686408 | tf_op jit(solution)/shard_map/ppermute | solution.py:111
  68.7 1.0 copy-start.2
  69.7 16.7 %collective-permute-start.3 = (bf16[600,1024]{1,0:T(8,128)(2,1)S(1)}, bf16[600,1024]{1,0:T(8,128)(2,1)S(1)}, u32[]{:S(2)}, u32[]{:S(2)}) collective-permute-start(bf16[600,1024]{1,0:T(8,128)(2,1)S(1)} %collective-permute-done.2), channel_id=1, source_target_pairs={{0,4},{4,8},{8,12},{12,14},{14,10},{10,6},{6,2},{2,0},{1,3},{5,1},... | collective-permute-start | bytes 3686408 | tf_op jit(solution)/shard_map/ppermute | solution.py:111
  86.5 1.0 copy-start.4
  87.5 16.8 %collective-permute-start.4 = (bf16[600,1024]{1,0:T(8,128)(2,1)S(1)}, bf16[600,1024]{1,0:T(8,128)(2,1)}, u32[]{:S(2)}, u32[]{:S(2)}) collective-permute-start(bf16[600,1024]{1,0:T(8,128)(2,1)S(1)} %collective-permute-done.3), channel_id=1, source_target_pairs={{0,4},{4,8},{8,12},{12,14},{14,10},{10,6},{6,2},{2,0},{1,3},{5,1},... | collective-permute-start | bytes 3686408 | tf_op jit(solution)/shard_map/ppermute | solution.py:111
  104.3 24.3 %collective-permute-start.5 = (bf16[600,1024]{1,0:T(8,128)(2,1)}, bf16[600,1024]{1,0:T(8,128)(2,1)}, u32[]{:S(2)}, u32[]{:S(2)}) collective-permute-start(bf16[600,1024]{1,0:T(8,128)(2,1)} %collective-permute-done.4), channel_id=1, source_target_pairs={{0,4},{4,8},{8,12},{12,14},{14,10},{10,6},{6,2},{2,0},{1,3},{5,1},... | collective-permute-start | bytes 3686408 | tf_op jit(solution)/shard_map/ppermute | solution.py:111
  128.6 17.2 %collective-permute-start.6 = (bf16[600,1024]{1,0:T(8,128)(2,1)}, bf16[600,1024]{1,0:T(8,128)(2,1)S(1)}, u32[]{:S(2)}, u32[]{:S(2)}) collective-permute-start(bf16[600,1024]{1,0:T(8,128)(2,1)} %collective-permute-done.5), channel_id=1, source_target_pairs={{0,4},{4,8},{8,12},{12,14},{14,10},{10,6},{6,2},{2,0},{1,3},{5,1},... | collective-permute-start | bytes 3686408 | tf_op jit(solution)/shard_map/ppermute | solution.py:111
  132.9 1.8 copy-start.3
  133.0 1.9 copy-start.5
  145.9 3.8 %copy-start = (bf16[600,8192]{1,0:T(8,128)(2,1)}, bf16[600,8192]{1,0:T(8,128)(2,1)S(1)}, u32[]{:S(2)}) copy-start(bf16[600,8192]{1,0:T(8,128)(2,1)S(1)} %constant_dynamic-update-slice_fusion) | copy-start | bytes 29491204
  145.9 3.8 %copy-start.11 = (f32[8192]{0:T(1024)S(1)}, f32[8192]{0:T(1024)}, u32[]{:S(2)}) copy-start(f32[8192]{0:T(1024)} %param.12) | copy-start | bytes 98308
  158.4 6.3 %collective-permute-start.7 = (bf16[600,128]{0,1:T(8,128)(2,1)S(1)}, bf16[600,128]{0,1:T(8,128)(2,1)S(1)}, u32[]{:S(2)}, u32[]{:S(2)}) collective-permute-start(bf16[600,128]{0,1:T(8,128)(2,1)S(1)} %get-tuple-element.29), channel_id=1, source_target_pairs={{0,2},{2,6},{4,10},{6,14},{8,0},{10,4},{12,8},{14,12},{1,3},{3,7},... | collective-permute-start | bytes 460808 | tf_op jit(solution)/shard_map/ppermute | solution.py:129
  158.5 6.2 %collective-permute-start.8 = (bf16[600,128]{0,1:T(8,128)(2,1)S(1)}, bf16[600,128]{0,1:T(8,128)(2,1)S(1)}, u32[]{:S(2)}, u32[]{:S(2)}) collective-permute-start(bf16[600,128]{0,1:T(8,128)(2,1)S(1)} %get-tuple-element.30), channel_id=1, source_target_pairs={{0,0},{2,4},{4,8},{6,12},{8,2},{10,6},{12,10},{14,14},{1,1},{3,5},... | collective-permute-start | bytes 460808 | tf_op jit(solution)/shard_map/ppermute | solution.py:128
  192.5 11.9 %copy-start.10 = (bf16[1024,8192]{1,0:T(8,128)(2,1)S(1)}, bf16[1024,8192]{1,0:T(8,128)(2,1)}, u32[]{:S(2)}) copy-start(bf16[1024,8192]{1,0:T(8,128)(2,1)} %all-gather.8.cloned.1.call-done) | copy-start | bytes 50331652
  196.1 19.5 %collective-permute-start.9 = (bf16[600,1024]{1,0:T(8,128)(2,1)S(1)}, bf16[600,1024]{1,0:T(8,128)(2,1)S(1)}, u32[]{:S(2)}, u32[]{:S(2)}) collective-permute-start(bf16[600,1024]{1,0:T(8,128)(2,1)S(1)} %fusion.28), channel_id=1, source_target_pairs={{0,4},{4,8},{8,12},{12,14},{14,10},{10,6},{6,2},{2,0},{1,3},{5,1},... | collective-permute-start | bytes 3686408 | tf_op jit(solution)/shard_map/ppermute | solution.py:159
  204.4 2.9 copy-start.13
  216.0 16.8 %collective-permute-start.10 = (bf16[600,1024]{1,0:T(8,128)(2,1)S(1)}, bf16[600,1024]{1,0:T(8,128)(2,1)S(1)}, u32[]{:S(2)}, u32[]{:S(2)}) collective-permute-start(bf16[600,1024]{1,0:T(8,128)(2,1)S(1)} %add_convert_fusion.6), channel_id=1, source_target_pairs={{0,4},{4,8},{8,12},{12,14},{14,10},{10,6},{6,2},{2,0},{1,3},{5,1},... | collective-permute-start | bytes 3686408 | tf_op jit(solution)/shard_map/ppermute | solution.py:159
  233.2 16.8 %collective-permute-start.11 = (bf16[600,1024]{1,0:T(8,128)(2,1)S(1)}, bf16[600,1024]{1,0:T(8,128)(2,1)S(1)}, u32[]{:S(2)}, u32[]{:S(2)}) collective-permute-start(bf16[600,1024]{1,0:T(8,128)(2,1)S(1)} %add_convert_fusion.5), channel_id=1, source_target_pairs={{0,4},{4,8},{8,12},{12,14},{14,10},{10,6},{6,2},{2,0},{1,3},{5,1},... | collective-permute-start | bytes 3686408 | tf_op jit(solution)/shard_map/ppermute | solution.py:159
  250.5 16.8 %collective-permute-start.12 = (bf16[600,1024]{1,0:T(8,128)(2,1)S(1)}, bf16[600,1024]{1,0:T(8,128)(2,1)S(1)}, u32[]{:S(2)}, u32[]{:S(2)}) collective-permute-start(bf16[600,1024]{1,0:T(8,128)(2,1)S(1)} %add_convert_fusion.4), channel_id=1, source_target_pairs={{0,4},{4,8},{8,12},{12,14},{14,10},{10,6},{6,2},{2,0},{1,3},{5,1},... | collective-permute-start | bytes 3686408 | tf_op jit(solution)/shard_map/ppermute | solution.py:159
  267.7 16.8 %collective-permute-start.13 = (bf16[600,1024]{1,0:T(8,128)(2,1)S(1)}, bf16[600,1024]{1,0:T(8,128)(2,1)S(1)}, u32[]{:S(2)}, u32[]{:S(2)}) collective-permute-start(bf16[600,1024]{1,0:T(8,128)(2,1)S(1)} %add_convert_fusion.3), channel_id=1, source_target_pairs={{0,4},{4,8},{8,12},{12,14},{14,10},{10,6},{6,2},{2,0},{1,3},{5,1},... | collective-permute-start | bytes 3686408 | tf_op jit(solution)/shard_map/ppermute | solution.py:159
  284.9 16.8 %collective-permute-start.14 = (bf16[600,1024]{1,0:T(8,128)(2,1)S(1)}, bf16[600,1024]{1,0:T(8,128)(2,1)S(1)}, u32[]{:S(2)}, u32[]{:S(2)}) collective-permute-start(bf16[600,1024]{1,0:T(8,128)(2,1)S(1)} %add_convert_fusion.2), channel_id=1, source_target_pairs={{0,4},{4,8},{8,12},{12,14},{14,10},{10,6},{6,2},{2,0},{1,3},{5,1},... | collective-permute-start | bytes 3686408 | tf_op jit(solution)/shard_map/ppermute | solution.py:159
  302.2 16.8 %collective-permute-start.15 = (bf16[600,1024]{1,0:T(8,128)(2,1)S(1)}, bf16[600,1024]{1,0:T(8,128)(2,1)S(1)}, u32[]{:S(2)}, u32[]{:S(2)}) collective-permute-start(bf16[600,1024]{1,0:T(8,128)(2,1)S(1)} %add_convert_fusion.1), channel_id=1, source_target_pairs={{0,4},{4,8},{8,12},{12,14},{14,10},{10,6},{6,2},{2,0},{1,3},{5,1},... | collective-permute-start | bytes 3686408 | tf_op jit(solution)/shard_map/ppermute | solution.py:159
Sparse Core Ops, SparseCore 0:
  8.9 16.3 all-gather.3
  26.8 31.2 all-gather.5
  59.7 31.2 all-gather.7
